TPU v7x, 256 devices: a whole 4x4x8 slice. The times are simulated.
256 devices in a mesh: ctx: 16 (over z_lo, y), dp: 16 (over x, z_hi, core).
Axes of the slice: x: 4, y: 4, z: 8 (z_hi: 2, z_lo: 4; z = z_hi * 4 + z_lo), core: 2. Of those that a mesh axis runs over, the one named last changes fastest.
Arguments:
- inputs: bfloat16 [16, 2048, 4096], P('dp', 'ctx'), may hold values from -6 to 6
- b_proj: bfloat16 [16, 2048, 512], P('dp', 'ctx'), may hold values from -0.75 to 0.75
- c_proj: bfloat16 [16, 2048, 512], P('dp', 'ctx'), may hold values from -0.75 to 0.75
- dt_raw: float32 [16, 64, 2048], P('dp', None, 'ctx'), may hold values from -3 to 9
- a_log: float32 [64], P('dp'), may hold values from -12 to -3
- dt_bias: float32 [64], P('dp'), may hold values from 0.2 to 0.8
- d_skip: float32 [64], P('dp'), may hold values from 0.5 to 1.5
- grad_out: bfloat16 [16, 2048, 4096], P('dp', 'ctx'), may hold values from -6 to 6
Outputs:
- grad_inputs: bfloat16 [16, 2048, 4096], P('dp', 'ctx')
- grad_b: bfloat16 [16, 2048, 512], P('dp', 'ctx')
- grad_c: bfloat16 [16, 2048, 512], P('dp', 'ctx')
- grad_dt: float32 [16, 64, 2048], P('dp', None, 'ctx')
- grad_alog: float32 [64], P('dp')
- grad_bias: float32 [64], P('dp')
- grad_skip: float32 [64], P('dp')
All inputs are finite; a program needn't handle non-finite values.
Results may differ from a plain program's by a relative error of at most 0.0014.
Values sent between devices are 32-bit elements; how exact they have to be, the bound alone decides.
No kernel may reach another device: no remote copies, remote signals or barrier semaphores. Data moves between devices by JAX's collectives and lax.ppermute only.
A program may use at most 192 MiB of HBM per device.

v0:
```python
import jax
import jax.numpy as jnp
from jax import lax
from jax.sharding import PartitionSpec as P

P_SIZE = 64
N = 64
G = 8


highest = lax.Precision.HIGHEST
fast = lax.Precision.HIGH


def slab_prelude(x, raw, bias, alog):
    tokens, num_heads, width = x.shape
    dt_value = jax.nn.softplus(raw + bias[:, None])
    log_decay = dt_value * (-jnp.exp(alog))[:, None]
    cumulative = jnp.cumsum(log_decay, axis=1)
    scaled = (x * dt_value.T[:, :, None]).reshape(tokens, G, num_heads // G, width)
    return cumulative, scaled


def slab_local(x, b, c, raw, bias, alog, skip):
    tokens, num_heads, width = x.shape
    group_heads = num_heads // G
    cumulative, scaled = slab_prelude(x, raw, bias, alog)
    scores = jnp.einsum("qgn,kgn->gqk", c, b, precision=fast)
    offsets = jnp.arange(tokens)
    causal = offsets[:, None] >= offsets[None, :]
    spread = cumulative[:, :, None] - cumulative[:, None, :]
    weights = jnp.where(causal, jnp.exp(jnp.where(causal, spread, 0.0)), 0.0)
    mixed = weights.reshape(G, group_heads, tokens, tokens) * scores[:, None]
    local_part = jnp.einsum("gjqk,kgjp->qgjp", mixed, scaled, precision=fast)
    return local_part.reshape(tokens, num_heads, width) + skip[None, :, None] * x


def slab_carry(x, b, c, raw, bias, alog, state_in):
    tokens, num_heads, width = x.shape
    group_heads = num_heads // G
    cumulative, scaled = slab_prelude(x, raw, bias, alog)
    tail_decay = jnp.exp(cumulative[:, -1:] - cumulative)
    weighted_b = b[:, :, None, :] * tail_decay.T.reshape(tokens, G, group_heads)[:, :, :, None]
    block_state = jnp.einsum("kgjn,kgjp->gjpn", weighted_b, scaled, precision=fast)
    block_state = block_state.reshape(num_heads, width, N)
    state_out = jnp.exp(cumulative[:, -1])[:, None, None] * state_in + block_state
    entering = state_in.reshape(G, group_heads, width, N)
    cross_part = jnp.einsum("qgn,gjpn->qgjp", c, entering, precision=fast)
    cross_part = cross_part * jnp.exp(cumulative).T.reshape(tokens, G, group_heads)[:, :, :, None]
    return (cross_part.reshape(tokens, num_heads, width), state_out)


def slab_terms(x, b, c, raw, bias, alog, grad):
    tokens, num_heads, width = x.shape
    group_heads = num_heads // G
    dt_value = jax.nn.softplus(raw + bias[:, None])
    log_decay = dt_value * (-jnp.exp(alog))[:, None]
    cumulative = jnp.cumsum(log_decay, axis=1)
    total = cumulative[:, -1]
    tail_decay = jnp.exp(total[:, None] - cumulative)
    carried = (x * (dt_value * tail_decay).T[:, :, None]).reshape(tokens, G, group_heads, width)
    local_state = jnp.einsum("tgn,tgjp->gjpn", b, carried, precision=fast)
    weighted_grad = (grad * jnp.exp(cumulative).T[:, :, None]).reshape(tokens, G, group_heads, width)
    local_source = jnp.einsum("tgn,tgjp->gjpn", c, weighted_grad, precision=fast)
    return (
        total,
        local_state.reshape(num_heads, width, N),
        local_source.reshape(num_heads, width, N),
    )


def carry_across(total, local_state, local_source, held):
    count = lax.axis_size("ctx")
    num_heads, width, lanes = local_state.shape
    share = num_heads // count
    rows = width * lanes // 128
    block = share * rows
    states = local_state.reshape(count, block, 128)
    sources = local_source.reshape(count, block, 128)
    totals = jnp.broadcast_to(total.reshape(count, share, 1), (count, share, 128))
    padding = -share % 8
    if padding:
        totals = jnp.concatenate([totals, jnp.zeros((count, padding, 128), totals.dtype)], axis=1)
    payload = jnp.concatenate([states, sources, totals], axis=1)
    chunk = payload.shape[1]
    got = lax.all_to_all(payload.reshape(count * chunk, 128), "ctx", 0, 0, tiled=True)
    got, held = lax.optimization_barrier((got, held))
    got = got.reshape(count, chunk, 128)
    states = got[:, :block].reshape(count * share, rows, 128)
    sources = got[:, block : 2 * block].reshape(count * share, rows, 128)
    totals = got[:, 2 * block : 2 * block + share, 0]
    slab = jnp.arange(count)
    between = (slab[None, :, None] < slab[None, None, :]) & (slab[None, None, :] < slab[:, None, None])
    exponent = jnp.einsum("jim,mh->jih", between.astype(jnp.float32), totals, precision=highest)
    before = slab[None, :] < slab[:, None]
    chain = jnp.where(before[:, :, None], jnp.exp(jnp.where(before[:, :, None], exponent, 0.0)), 0.0)
    same = jnp.eye(share, dtype=chain.dtype)
    spread = (chain[:, :, :, None] * same[None, None]).transpose(0, 2, 1, 3)
    spread = spread.reshape(count * share, count * share)
    entering = jnp.einsum("ab,brl->arl", spread, states, precision=highest)
    leaving = jnp.einsum("ba,brl->arl", spread, sources, precision=highest)
    back = jnp.concatenate(
        [entering.reshape(count, block, 128), leaving.reshape(count, block, 128)], axis=1
    )
    mine = lax.all_to_all(back.reshape(count * 2 * block, 128), "ctx", 0, 0, tiled=True)
    mine = mine.reshape(count, 2 * block, 128)
    entering = mine[:, :block].reshape(num_heads, width, lanes)
    leaving = mine[:, block:].reshape(num_heads, width, lanes)
    return entering, leaving, held


def exchange(value, axis, distance):
    count = lax.axis_size(axis)
    return lax.ppermute(value, axis, [(i, i ^ distance) for i in range(count)])


def group_values(value, axis, stride):
    place = (lax.axis_index(axis) // stride) % 4
    held = [value] + [exchange(value, axis, step * stride) for step in (1, 2, 3)]
    ordered = []
    for position in range(4):
        pick = held[3]
        for step in (2, 1, 0):
            pick = jnp.where((place ^ step) == position, held[step], pick)
        ordered.append(pick)
    return ordered


def gather_by_doubling(value, axis):
    stride = 1
    while stride < lax.axis_size(axis):
        value = jnp.concatenate(group_values(value, axis, stride), axis=-1)
        stride *= 4
    return value


def sum_by_butterfly(value, axes):
    for axis in axes:
        stride = 1
        while stride < lax.axis_size(axis):
            first, second, third, fourth = group_values(value, axis, stride)
            value = (first + second) + (third + fourth)
            stride *= 4
    return value


def per_device(inputs, b_proj, c_proj, dt_raw, a_log, dt_bias, d_skip, grad_out):
    params = gather_by_doubling(jnp.stack([a_log, dt_bias, d_skip]), "dp")
    alog_all, bias_all, skip_all = params[0], params[1], params[2]
    tokens = inputs.shape[1]
    num_heads = alog_all.shape[0]
    x = inputs[0].astype(jnp.float32).reshape(tokens, num_heads, P_SIZE)
    grad = grad_out[0].astype(jnp.float32).reshape(tokens, num_heads, P_SIZE)
    b = b_proj[0].astype(jnp.float32).reshape(tokens, G, N)
    c = c_proj[0].astype(jnp.float32).reshape(tokens, G, N)
    raw = dt_raw[0]
    total, local_state, local_source = slab_terms(x, b, c, raw, bias_all, alog_all, grad)
    (total, local_state, local_source), late = lax.optimization_barrier(
        ((total, local_state, local_source), (x, b, c, raw, bias_all, alog_all, skip_all, grad))
    )
    _, local_pullback = jax.vjp(slab_local, *late[:7])
    local_grads = local_pullback(late[7])
    entering, leaving, local_grads = carry_across(total, local_state, local_source, local_grads)
    _, carry_pullback = jax.vjp(slab_carry, x, b, c, raw, bias_all, alog_all, entering)
    carry_grads = carry_pullback((grad, leaving))[:6]
    gx, gb, gc, graw, gbias, galog = [u + v for u, v in zip(local_grads[:6], carry_grads)]
    gskip = local_grads[6]
    grad_inputs = gx.reshape(tokens, num_heads * P_SIZE).astype(jnp.bfloat16)[None]
    grad_b = gb.reshape(tokens, G * N).astype(jnp.bfloat16)[None]
    grad_c = gc.reshape(tokens, G * N).astype(jnp.bfloat16)[None]
    grad_dt = graw[None]
    head_stats = jnp.stack([galog, gbias, gskip], axis=0)
    count = lax.axis_size("dp")
    share_size = num_heads // count
    dealt = head_stats.reshape(3, count, share_size).transpose(1, 0, 2)
    own_totals = jnp.sum(lax.all_to_all(dealt, "dp", 0, 0, tiled=True), axis=0)
    own_totals = sum_by_butterfly(own_totals, ("ctx",))
    return (grad_inputs, grad_b, grad_c, grad_dt, own_totals[0], own_totals[1], own_totals[2])


def solution(mesh):
    in_specs = (
        P("dp", "ctx", None),
        P("dp", "ctx", None),
        P("dp", "ctx", None),
        P("dp", None, "ctx"),
        P("dp"),
        P("dp"),
        P("dp"),
        P("dp", "ctx", None),
    )
    out_specs = (
        P("dp", "ctx", None),
        P("dp", "ctx", None),
        P("dp", "ctx", None),
        P("dp", None, "ctx"),
        P("dp"),
        P("dp"),
        P("dp"),
    )
    return jax.shard_map(
        per_device, mesh=mesh, in_specs=in_specs, out_specs=out_specs, check_vma=False
    )
```

profile of v0, /device:TPU:2, one launch (start us, length us, event | category | flops | bytes accessed | tf_op | source)
XLA Modules:
  0.0 223.7 jit_solution(16151595028769599835)
XLA Ops:
  2.0 6.6 %collective-permute-start.2 = (f32[3,4]{1,0:T(4,128)}, f32[3,4]{1,0:T(4,128)S(1)}, u32[]{:S(2)}, u32[]{:S(2)}) collective-permute-start(f32[3,4]{1,0:T(4,128)} %pad_maximum_fusion.1), channel_id=1, source_target_pairs={{0,3},{1,2},{2,1},{3,0},{4,7},{5,6},{6,5},{7,4},{8,11},{9,10},{10,... | collective-permute-start | bytes 152 | tf_op jit(solution)/shard_map/ppermute | solution.py:114
  25.8 3.1 %fusion.27 = f32[8,8,64,64]{3,2,1,0:T(8,128)} fusion(bf16[128,8,64,1]{0,2,3,1:T(8,128)(2,1)} %bitcast.229, f32[128,8,8,64]{0,3,2,1:T(8,128)S(1)} %bitcast.207, f32[128,8,8]{0,2,1:T(8,128)S(1)} %get-tuple-element.121), kind=kOutput, calls=%fused_computation.39 | convolution fusion | flops 201850880 | bytes 3309568 | tf_op jit(solution)/shard_map/tgn,tgjp->gjpn/dot_general | solution.py:62
  33.5 2.6 %reshape.316 = f32[16,128,128]{2,1,0:T(8,128)} reshape(f32[64,64,64]{2,1,0:T(8,128)} %bitcast.217) | data formatting | bytes 2097152 | tf_op jit(solution)/shard_map/reshape | solution.py:79
  36.1 2.9 %maximum_maximum_fusion = f32[16,264,128]{2,1,0:T(8,128)} fusion(f32[16,4,128]{2,1,0:T(4,128)S(1)} %broadcast_in_dim.46, f32[16,128,128]{2,1,0:T(8,128)} %reshape.316, f32[16,128,128]{2,1,0:T(8,128)S(1)} %reshape.315, f32[264]{0:T(512)S(1)} %pad.16.clone), kind=kLoop, calls=%fused_computation.8 | loop fusion | flops 1622016 | bytes 4293664 | tf_op jit(solution)/shard_map/concatenate | solution.py:84
  39.0 7.1 %all-to-all-start = ((f32[16,264,128]{2,1,0:T(8,128)}), f32[16,264,128]{2,1,0:T(8,128)}, u32[]{:S(2)}, u32[]{:S(2)}) async-start(f32[16,264,128]{2,1,0:T(8,128)} %maximum_maximum_fusion), calls=%async_computation | async-start | bytes 4325376 | tf_op jit(solution)/shard_map/all_to_all | solution.py:86
  49.2 4.7 %fusion = f32[8,8,64,128]{3,2,1,0:T(8,128)S(1)} fusion(f32[8,8,64,128]{3,2,1,0:T(8,128)} %bitcast.211, f32[8,128,128]{2,1,0:T(8,128)S(1)} %fusion.77, f32[8,8,128]{2,1,0:T(8,128)S(1)} %reduce_window_sum.45, pred[128,128]{1,0:T(8,128)(4,1)S(1)} %iota_compare_fusion), kind=kOutput, calls=%fused_computation.2 | convolution fusion | flops 406847488 | bytes 4767744 | tf_op jit(solution)/shard_map/transpose(jvp(gjqk,kgjp->qgjp))/dot_general | solution.py:34
  56.4 6.5 %fusion.5 = (f32[8,8,128]{2,1,0:T(8,128)S(1)}, f32[8,8,128]{2,1,0:T(8,128)S(1)}, f32[8,128,128]{2,1,0:T(8,128)S(1)}) fusion(f32[8,128,128]{2,1,0:T(8,128)S(1)} %fusion.77, f32[8,8,128]{2,1,0:T(8,128)S(1)} %reduce_window_sum.45, pred[128,128]{1,0:T(8,128)(4,1)S(1)} %iota_compare_fusion, f32[8,8,64,128]{3,2,1,0:T(8,128)S(1)} %bitcast.216, ...), kind=kOutput, calls=%fused_computation.7 | convolution fusion | flops 414040064 | bytes 5357568 | tf_op jit(solution)/shard_map/transpose(jvp(gjqk,kgjp->qgjp))/dot_general | solution.py:34
  68.4 20.7 %all-to-all-done = f32[16,264,128]{2,1,0:T(8,128)} async-done(((f32[16,264,128]{2,1,0:T(8,128)}), f32[16,264,128]{2,1,0:T(8,128)}, u32[]{:S(2)}, u32[]{:S(2)}) %all-to-all-start) | async-done | bytes 2162720 | tf_op jit(solution)/shard_map/all_to_all | solution.py:86
  90.0 3.1 %fusion.76 = (f32[16,128,128]{2,1,0:T(8,128)}, f32[16,128,128]{2,1,0:T(8,128)}) fusion(f32[16,264,128]{2,1,0:T(8,128)} %bitcast.37), kind=kLoop, calls=%fused_computation.138 | loop fusion | bytes 4194304 | tf_op jit(solution)/shard_map/slice | solution.py:89
  94.5 2.9 %fusion.44 = f32[64,32,128]{2,0,1:T(8,128)S(1)} fusion(f32[64,64,1]{1,0,2:T(8,128)S(1)} %reshape.336, f32[64,32,128]{2,1,0:T(8,128)} %bitcast.221), kind=kOutput, calls=%fused_computation.53 | convolution fusion | flops 201326592 | bytes 2113536 | tf_op jit(solution)/shard_map/ab,brl->arl/dot_general | solution.py:100
  101.8 10.9 %all-to-all-start.1 = ((f32[16,256,128]{2,1,0:T(8,128)}), f32[16,256,128]{2,1,0:T(8,128)}, u32[]{:S(2)}, u32[]{:S(2)}) async-start(f32[16,256,128]{2,1,0:T(8,128)} %pad_maximum_fusion), calls=%async_computation.1 | async-start | bytes 4194304 | tf_op jit(solution)/shard_map/all_to_all | solution.py:105
  113.6 41.2 %all-to-all-done.1 = f32[16,256,128]{2,1,0:T(8,128)} async-done(((f32[16,256,128]{2,1,0:T(8,128)}), f32[16,256,128]{2,1,0:T(8,128)}, u32[]{:S(2)}, u32[]{:S(2)}) %all-to-all-start.1) | async-done | bytes 2097184 | tf_op jit(solution)/shard_map/all_to_all | solution.py:105
  154.8 3.2 %slice_multiply_fusion = (f32[16,128,128]{2,1,0:T(8,128)}, f32[16,128,128]{2,1,0:T(8,128)}, f32[16,128,128]{2,1,0:T(8,128)S(1)}) fusion(f32[16,256,128]{2,1,0:T(8,128)} %all-to-all-done.1), kind=kLoop, calls=%fused_computation.133 | loop fusion | flops 262144 | bytes 5242880 | tf_op jit(solution)/shard_map/transpose(jvp())/mul | solution.py:46
  158.0 2.7 %mul.284 = f32[64,64,64]{2,1,0:T(8,128)} reshape(f32[16,128,128]{2,1,0:T(8,128)} %get-tuple-element.110) | data formatting | bytes 2097152 | tf_op jit(solution)/shard_map/transpose(jvp())/mul | solution.py:46
  160.8 2.7 %reduce_sum.167 = f32[64]{0:T(128)} reduce(f32[64,64,64]{2,1,0:T(8,128)} %mul.284, f32[]{:T(128)} %constant.91.clone.1), dimensions={1,2}, to_apply=%region_14.16 | reduce | flops 262080 | bytes 1048836 | tf_op jit(solution)/shard_map/transpose(jvp())/reduce_sum | solution.py:46
  167.7 2.7 %reshape_reshape.8 = f32[8,8,64,64]{3,2,1,0:T(8,128)} reshape(f32[16,128,128]{2,1,0:T(8,128)} %get-tuple-element.111) | data formatting | bytes 2097152 | tf_op jit(solution)/shard_map/jvp()/reshape;reshape | solution.py:47
  170.4 3.6 %fusion.8 = f32[128,8,8]{0,2,1:T(8,128)} fusion(f32[128,8,8,64]{0,3,2,1:T(8,128)} %bitcast.212, f32[8,8,64,64]{3,2,1,0:T(8,128)} %reshape_reshape.8, bf16[128,8,64,1]{0,2,3,1:T(8,128)(2,1)S(1)} %bitcast.226), kind=kOutput, calls=%fused_computation.14 | convolution fusion | flops 202366976 | bytes 3309568 | tf_op jit(solution)/shard_map/jvp(qgn,gjpn->qgjp)/dot_general | solution.py:48
  176.6 4.4 %fusion.13 = (f32[128,8,8]{0,2,1:T(8,128)S(1)}, f32[8,8,64,128]{3,2,1,0:T(8,128)}) fusion(f32[128,8,8,64]{0,3,2,1:T(8,128)S(1)} %bitcast.209, f32[8,8,64,64]{3,2,1,0:T(8,128)} %reshape_reshape.7, f32[128,8,8]{0,2,1:T(8,128)S(1)} %bitcast.234, f32[128,8,64]{0,2,1:T(8,128)S(1)} %convert_element_type.94), kind=kOutput, calls=%fused_computation.22 | convolution fusion | flops 202891264 | bytes 5570560 | tf_op jit(solution)/shard_map/transpose(jvp(kgjn,kgjp->gjpn))/dot_general | solution.py:44
  186.3 9.0 %all-to-all-start.2 = ((f32[16,3,4]{2,1,0:T(4,128)}), f32[16,3,4]{2,1,0:T(4,128)S(1)}, u32[]{:S(2)}, u32[]{:S(2)}) async-start(f32[16,3,4]{2,1,0:T(4,128)} %copy.133), calls=%async_computation.2 | async-start | bytes 65536 | tf_op jit(solution)/shard_map/all_to_all | solution.py:176
  195.4 4.3 %fusion.36 = bf16[128,8,64]{0,2,1:T(8,128)(2,1)S(1)} fusion(f32[128,8,64]{0,2,1:T(8,128)S(1)} %copy-done.10, f32[8,8,64,64]{3,2,1,0:T(8,128)} %reshape_reshape.8, f32[128,8,8,64]{0,3,2,1:T(8,128)} %bitcast.213, f32[128,8,8]{0,2,1:T(8,128)S(1)} %bitcast.236), kind=kOutput, calls=%fused_computation.46 | convolution fusion | flops 201981952 | bytes 3571712 | tf_op jit(solution)/shard_map/transpose(jvp(qgn,gjpn->qgjp))/dot_general | solution.py:48
  204.0 3.7 %collective-permute-start.8 = (f32[3,4]{1,0:T(4,128)S(1)}, f32[3,4]{1,0:T(4,128)S(1)}, u32[]{:S(2)}, u32[]{:S(2)}) collective-permute-start(f32[3,4]{1,0:T(4,128)S(1)} %reduce_sum.176), channel_id=1, source_target_pairs={{0,48},{16,32},{32,16},{48,0},{64,112},{80,96},{96,80},{112,64},{1... | collective-permute-start | bytes 152 | tf_op jit(solution)/shard_map/ppermute | solution.py:114
  209.3 3.5 %collective-permute-done.7 = f32[3,4]{1,0:T(4,128)S(1)} collective-permute-done((f32[3,4]{1,0:T(4,128)S(1)}, f32[3,4]{1,0:T(4,128)S(1)}, u32[]{:S(2)}, u32[]{:S(2)}) %collective-permute-start.7) | collective-permute-done | bytes 80 | tf_op jit(solution)/shard_map/ppermute | solution.py:114
  212.8 5.8 %collective-permute-start.11 = (f32[3,4]{1,0:T(4,128)S(1)}, f32[3,4]{1,0:T(4,128)S(1)}, u32[]{:S(2)}, u32[]{:S(2)}) collective-permute-start(f32[3,4]{1,0:T(4,128)S(1)} %add_add_fusion.1), channel_id=1, source_target_pairs={{0,192},{16,208},{32,224},{48,240},{64,128},{80,144},{96,160},{112... | collective-permute-start | bytes 152 | tf_op jit(solution)/shard_map/ppermute | solution.py:114
  220.2 2.9 %collective-permute-done.10 = f32[3,4]{1,0:T(4,128)S(1)} collective-permute-done((f32[3,4]{1,0:T(4,128)S(1)}, f32[3,4]{1,0:T(4,128)S(1)}, u32[]{:S(2)}, u32[]{:S(2)}) %collective-permute-start.10) | collective-permute-done | bytes 80 | tf_op jit(solution)/shard_map/ppermute | solution.py:114
  (165 shorter events, 61.6 us)
Async XLA Ops:
  0.6 11.6 %copy-start.9 = (bf16[1,128,4096]{2,1,0:T(8,128)(2,1)S(1)}, bf16[1,128,4096]{2,1,0:T(8,128)(2,1)}, u32[]{:S(2)}) copy-start(bf16[1,128,4096]{2,1,0:T(8,128)(2,1)} %param.9) | copy-start | bytes 3145732
  2.0 14.1 %collective-permute-start.2 = (f32[3,4]{1,0:T(4,128)}, f32[3,4]{1,0:T(4,128)S(1)}, u32[]{:S(2)}, u32[]{:S(2)}) collective-permute-start(f32[3,4]{1,0:T(4,128)} %pad_maximum_fusion.1), channel_id=1, source_target_pairs={{0,3},{1,2},{2,1},{3,0},{4,7},{5,6},{6,5},{7,4},{8,11},{9,10},{10,... | collective-permute-start | bytes 152 | tf_op jit(solution)/shard_map/ppermute | solution.py:114
  8.6 7.7 %collective-permute-start.1 = (f32[3,4]{1,0:T(4,128)}, f32[3,4]{1,0:T(4,128)S(1)}, u32[]{:S(2)}, u32[]{:S(2)}) collective-permute-start(f32[3,4]{1,0:T(4,128)} %pad_maximum_fusion.1), channel_id=1, source_target_pairs={{0,2},{1,3},{2,0},{3,1},{4,6},{5,7},{6,4},{7,5},{8,10},{9,11},{10,... | collective-permute-start | bytes 152 | tf_op jit(solution)/shard_map/ppermute | solution.py:114
  9.2 7.1 %collective-permute-start = (f32[3,4]{1,0:T(4,128)}, f32[3,4]{1,0:T(4,128)S(1)}, u32[]{:S(2)}, u32[]{:S(2)}) collective-permute-start(f32[3,4]{1,0:T(4,128)} %pad_maximum_fusion.1), channel_id=1, source_target_pairs={{0,1},{1,0},{2,3},{3,2},{4,5},{5,4},{6,7},{7,6},{8,9},{9,8},{10,11... | collective-permute-start | bytes 152 | tf_op jit(solution)/shard_map/ppermute | solution.py:114
  14.7 9.1 %copy-start.12 = (f32[1,64,128]{2,1,0:T(8,128)S(1)}, f32[1,64,128]{2,1,0:T(8,128)}, u32[]{:S(2)}) copy-start(f32[1,64,128]{2,1,0:T(8,128)} %param.12) | copy-start | bytes 98308
  16.5 4.2 %collective-permute-start.5 = (f32[3,16]{1,0:T(4,128)S(1)}, f32[3,16]{1,0:T(4,128)S(1)}, u32[]{:S(2)}, u32[]{:S(2)}) collective-permute-start(f32[3,16]{1,0:T(4,128)S(1)} %pad_maximum_fusion.2), channel_id=1, source_target_pairs={{0,12},{1,13},{2,14},{3,15},{4,8},{5,9},{6,10},{7,11},{8,4},{9,5},... | collective-permute-start | bytes 584 | tf_op jit(solution)/shard_map/ppermute | solution.py:114
  18.0 5.1 %collective-permute-start.4 = (f32[3,16]{1,0:T(4,128)S(1)}, f32[3,16]{1,0:T(4,128)S(1)}, u32[]{:S(2)}, u32[]{:S(2)}) collective-permute-start(f32[3,16]{1,0:T(4,128)S(1)} %pad_maximum_fusion.2), channel_id=1, source_target_pairs={{0,8},{1,9},{2,10},{3,11},{4,12},{5,13},{6,14},{7,15},{8,0},{9,1},... | collective-permute-start | bytes 584 | tf_op jit(solution)/shard_map/ppermute | solution.py:114
  19.1 4.0 %collective-permute-start.3 = (f32[3,16]{1,0:T(4,128)S(1)}, f32[3,16]{1,0:T(4,128)S(1)}, u32[]{:S(2)}, u32[]{:S(2)}) collective-permute-start(f32[3,16]{1,0:T(4,128)S(1)} %pad_maximum_fusion.2), channel_id=1, source_target_pairs={{0,4},{1,5},{2,6},{3,7},{4,0},{5,1},{6,2},{7,3},{8,12},{9,13},{10,... | collective-permute-start | bytes 584 | tf_op jit(solution)/shard_map/ppermute | solution.py:114
  23.2 5.7 %copy-start.20 = (f32[3,64]{1,0:T(4,128)}, f32[3,64]{1,0:T(4,128)S(1)}, u32[]{:S(2)}) copy-start(f32[3,64]{1,0:T(4,128)S(1)} %pad_maximum_fusion.3) | copy-start | bytes 2308
  39.0 7.2 %copy-start.31 = (f32[64]{0:T(128)S(1)}, f32[64]{0:T(128)}, u32[]{:S(2)}) copy-start(f32[64]{0:T(128)} %get-tuple-element.38) | copy-start | bytes 772
  39.0 7.2 %copy-start.13 = (f32[1,64,128]{2,1,0:T(8,128)S(1)}, f32[1,64,128]{2,1,0:T(8,128)}, u32[]{:S(2)}) copy-start(f32[1,64,128]{2,1,0:T(8,128)} %param.12) | copy-start | bytes 98308
  39.0 9.6 %copy-start.6 = (f32[128,8,64]{0,2,1:T(8,128)S(1)}, f32[128,8,64]{0,2,1:T(8,128)}, u32[]{:S(2)}) copy-start(f32[128,8,64]{0,2,1:T(8,128)} %convert_element_type.95) | copy-start | bytes 786436
  39.0 50.1 %all-to-all-start = ((f32[16,264,128]{2,1,0:T(8,128)}), f32[16,264,128]{2,1,0:T(8,128)}, u32[]{:S(2)}, u32[]{:S(2)}) async-start(f32[16,264,128]{2,1,0:T(8,128)} %maximum_maximum_fusion), calls=%async_computation | async-start | bytes 4325376 | tf_op jit(solution)/shard_map/all_to_all | solution.py:86
  101.8 11.0 %copy-start.16 = (f32[64,128]{1,0:T(8,128)S(1)}, f32[64,128]{1,0:T(8,128)}, u32[]{:S(2)}) copy-start(f32[64,128]{1,0:T(8,128)} %copy-done.15) | copy-start | bytes 98308
  101.8 53.0 %all-to-all-start.1 = ((f32[16,256,128]{2,1,0:T(8,128)}), f32[16,256,128]{2,1,0:T(8,128)}, u32[]{:S(2)}, u32[]{:S(2)}) async-start(f32[16,256,128]{2,1,0:T(8,128)} %pad_maximum_fusion), calls=%async_computation.1 | async-start | bytes 4194304 | tf_op jit(solution)/shard_map/all_to_all | solution.py:105
  181.0 14.3 %copy-start.11 = (f32[128,8,64]{0,2,1:T(8,128)S(1)}, f32[128,8,64]{0,2,1:T(8,128)}, u32[]{:S(2)}) copy-start(f32[128,8,64]{0,2,1:T(8,128)} %convolution_bitcast_fusion.1) | copy-start | bytes 786436
  181.0 14.3 %copy-start.10 = (f32[128,8,64]{0,2,1:T(8,128)S(1)}, f32[128,8,64]{0,2,1:T(8,128)}, u32[]{:S(2)}) copy-start(f32[128,8,64]{0,2,1:T(8,128)} %convolution_bitcast_fusion) | copy-start | bytes 786436
  186.3 17.7 %all-to-all-start.2 = ((f32[16,3,4]{2,1,0:T(4,128)}), f32[16,3,4]{2,1,0:T(4,128)S(1)}, u32[]{:S(2)}, u32[]{:S(2)}) async-start(f32[16,3,4]{2,1,0:T(4,128)} %copy.133), calls=%async_computation.2 | async-start | bytes 65536 | tf_op jit(solution)/shard_map/all_to_all | solution.py:176
  204.0 5.3 %collective-permute-start.8 = (f32[3,4]{1,0:T(4,128)S(1)}, f32[3,4]{1,0:T(4,128)S(1)}, u32[]{:S(2)}, u32[]{:S(2)}) collective-permute-start(f32[3,4]{1,0:T(4,128)S(1)} %reduce_sum.176), channel_id=1, source_target_pairs={{0,48},{16,32},{32,16},{48,0},{64,112},{80,96},{96,80},{112,64},{1... | collective-permute-start | bytes 152 | tf_op jit(solution)/shard_map/ppermute | solution.py:114
  207.7 5.1 %collective-permute-start.7 = (f32[3,4]{1,0:T(4,128)S(1)}, f32[3,4]{1,0:T(4,128)S(1)}, u32[]{:S(2)}, u32[]{:S(2)}) collective-permute-start(f32[3,4]{1,0:T(4,128)S(1)} %reduce_sum.176), channel_id=1, source_target_pairs={{0,32},{16,48},{32,0},{48,16},{64,96},{80,112},{96,64},{112,80},{1... | collective-permute-start | bytes 152 | tf_op jit(solution)/shard_map/ppermute | solution.py:114
  208.4 4.4 %collective-permute-start.6 = (f32[3,4]{1,0:T(4,128)S(1)}, f32[3,4]{1,0:T(4,128)S(1)}, u32[]{:S(2)}, u32[]{:S(2)}) collective-permute-start(f32[3,4]{1,0:T(4,128)S(1)} %reduce_sum.176), channel_id=1, source_target_pairs={{0,16},{16,0},{32,48},{48,32},{64,80},{80,64},{96,112},{112,96},{1... | collective-permute-start | bytes 152 | tf_op jit(solution)/shard_map/ppermute | solution.py:114
  212.8 7.3 %collective-permute-start.11 = (f32[3,4]{1,0:T(4,128)S(1)}, f32[3,4]{1,0:T(4,128)S(1)}, u32[]{:S(2)}, u32[]{:S(2)}) collective-permute-start(f32[3,4]{1,0:T(4,128)S(1)} %add_add_fusion.1), channel_id=1, source_target_pairs={{0,192},{16,208},{32,224},{48,240},{64,128},{80,144},{96,160},{112... | collective-permute-start | bytes 152 | tf_op jit(solution)/shard_map/ppermute | solution.py:114
  218.6 4.5 %collective-permute-start.10 = (f32[3,4]{1,0:T(4,128)S(1)}, f32[3,4]{1,0:T(4,128)S(1)}, u32[]{:S(2)}, u32[]{:S(2)}) collective-permute-start(f32[3,4]{1,0:T(4,128)S(1)} %add_add_fusion.1), channel_id=1, source_target_pairs={{0,128},{16,144},{32,160},{48,176},{64,192},{80,208},{96,224},{112... | collective-permute-start | bytes 152 | tf_op jit(solution)/shard_map/ppermute | solution.py:114
  219.6 3.6 %collective-permute-start.9 = (f32[3,4]{1,0:T(4,128)S(1)}, f32[3,4]{1,0:T(4,128)S(1)}, u32[]{:S(2)}, u32[]{:S(2)}) collective-permute-start(f32[3,4]{1,0:T(4,128)S(1)} %add_add_fusion.1), channel_id=1, source_target_pairs={{0,64},{16,80},{32,96},{48,112},{64,0},{80,16},{96,32},{112,48},{1... | collective-permute-start | bytes 152 | tf_op jit(solution)/shard_map/ppermute | solution.py:114
  (23 other events, 73.5 us)
where the time goes:
time: 225 us; the launch traced here: 224 us
  waiting for transfers between devices  72.2 us (32%)
  starting transfers between devices  49.9 us (22%)
  matrix products  38.6 us (17%)
  local copies, waits for them, and re-layouts  31.2 us (14%)
  other arithmetic  30.5 us (14%)
    all_to_all x1, waiting for transfers between devices, carry_across(): lax.all_to_all(back.reshape(count * 2 * block, 128), 'ctx', 0, 0, tiled=T...  41.2 us
    ppermute x12, starting transfers between devices, exchange(): return lax.ppermute(value, axis, [(i, i ^ distance) for i in range(count)])  22.9 us
    all_to_all x1, waiting for transfers between devices, carry_across(): lax.all_to_all(payload.reshape(count * chunk, 128), 'ctx', 0, 0, tiled=True)  20.7 us
    dot_general x2, matrix products, slab_local(): local_part = jnp.einsum('gjqk,kgjp->qgjp', mixed, scaled, precision=fast)  11.2 us
    all_to_all x1, starting transfers between devices, carry_across(): lax.all_to_all(back.reshape(count * 2 * block, 128), 'ctx', 0, 0, tiled=T...  10.9 us
    ppermute x12, waiting for transfers between devices, exchange(): return lax.ppermute(value, axis, [(i, i ^ distance) for i in range(count)])  10.3 us
    all_to_all x1, starting transfers between devices, per_device(): own_totals = jnp.sum(lax.all_to_all(dealt, 'dp', 0, 0, tiled=True), axis=0)  8.97 us
    dot_general x2, matrix products, slab_carry(): cross_part = jnp.einsum('qgn,gjpn->qgjp', c, entering, precision=fast)  7.93 us
  transfers between devices with their start and end apart: 15, of which 9 were waited for; matrix products, arithmetic and copies ran while one was open for 17% of the time, Pallas kernels for 0%

commit v1 on v0

--- a/solution.py
+++ b/solution.py
@@ -59,29 +59,28 @@
     total = cumulative[:, -1]
     tail_decay = jnp.exp(total[:, None] - cumulative)
     carried = (x * (dt_value * tail_decay).T[:, :, None]).reshape(tokens, G, group_heads, width)
-    local_state = jnp.einsum("tgn,tgjp->gjpn", b, carried, precision=fast)
     weighted_grad = (grad * jnp.exp(cumulative).T[:, :, None]).reshape(tokens, G, group_heads, width)
-    local_source = jnp.einsum("tgn,tgjp->gjpn", c, weighted_grad, precision=fast)
-    return (
-        total,
-        local_state.reshape(num_heads, width, N),
-        local_source.reshape(num_heads, width, N),
-    )
-
-
-def carry_across(total, local_state, local_source, held):
+    both = jnp.einsum(
+        "tgwn,tgwjp->wgjpn",
+        jnp.stack([b, c], axis=2),
+        jnp.stack([carried, weighted_grad], axis=2),
+        precision=fast,
+    )
+    return (total, both.reshape(2, num_heads, width, N))
+
+
+def carry_across(total, both, held):
     count = lax.axis_size("ctx")
-    num_heads, width, lanes = local_state.shape
+    _, num_heads, width, lanes = both.shape
     share = num_heads // count
     rows = width * lanes // 128
     block = share * rows
-    states = local_state.reshape(count, block, 128)
-    sources = local_source.reshape(count, block, 128)
+    pairs = both.reshape(2, count, block, 128).transpose(1, 0, 2, 3).reshape(count, 2 * block, 128)
     totals = jnp.broadcast_to(total.reshape(count, share, 1), (count, share, 128))
     padding = -share % 8
     if padding:
         totals = jnp.concatenate([totals, jnp.zeros((count, padding, 128), totals.dtype)], axis=1)
-    payload = jnp.concatenate([states, sources, totals], axis=1)
+    payload = jnp.concatenate([pairs, totals], axis=1)
     chunk = payload.shape[1]
     got = lax.all_to_all(payload.reshape(count * chunk, 128), "ctx", 0, 0, tiled=True)
     got, held = lax.optimization_barrier((got, held))
@@ -97,8 +96,8 @@
     same = jnp.eye(share, dtype=chain.dtype)
     spread = (chain[:, :, :, None] * same[None, None]).transpose(0, 2, 1, 3)
     spread = spread.reshape(count * share, count * share)
-    entering = jnp.einsum("ab,brl->arl", spread, states, precision=highest)
-    leaving = jnp.einsum("ba,brl->arl", spread, sources, precision=highest)
+    entering = jnp.einsum("ab,brl->arl", spread, states, precision=fast)
+    leaving = jnp.einsum("ba,brl->arl", spread, sources, precision=fast)
     back = jnp.concatenate(
         [entering.reshape(count, block, 128), leaving.reshape(count, block, 128)], axis=1
     )
@@ -154,13 +153,13 @@
     b = b_proj[0].astype(jnp.float32).reshape(tokens, G, N)
     c = c_proj[0].astype(jnp.float32).reshape(tokens, G, N)
     raw = dt_raw[0]
-    total, local_state, local_source = slab_terms(x, b, c, raw, bias_all, alog_all, grad)
-    (total, local_state, local_source), late = lax.optimization_barrier(
-        ((total, local_state, local_source), (x, b, c, raw, bias_all, alog_all, skip_all, grad))
+    total, both = slab_terms(x, b, c, raw, bias_all, alog_all, grad)
+    (total, both), late = lax.optimization_barrier(
+        ((total, both), (x, b, c, raw, bias_all, alog_all, skip_all, grad))
     )
     _, local_pullback = jax.vjp(slab_local, *late[:7])
     local_grads = local_pullback(late[7])
-    entering, leaving, local_grads = carry_across(total, local_state, local_source, local_grads)
+    entering, leaving, local_grads = carry_across(total, both, local_grads)
     _, carry_pullback = jax.vjp(slab_carry, x, b, c, raw, bias_all, alog_all, entering)
     carry_grads = carry_pullback((grad, leaving))[:6]
     gx, gb, gc, graw, gbias, galog = [u + v for u, v in zip(local_grads[:6], carry_grads)]

time: 225 us -> 228 us (1.013)
  other arithmetic: 30.5 us -> 33.6 us
  matrix products: 38.6 us -> 35.8 us
  local copies, waits for them, and re-layouts: 31.2 us -> 34 us
    transpose x0 -> x1, local copies, waits for them, and re-layouts: none -> 3.13 us  [carry_across(): both.reshape(2, count, block, 128).transpose(1, 0, 2, 3)]
    dot_general x4 -> x3, matrix products: 9.61 us -> 6.83 us  [the longest x1 3.23 us: slab_terms(): jnp.einsum('tgwn,tgwjp->wgjpn', jnp.stack([b, c], axis=2), jnp.stack([car...]
    mul x0 -> x1, other arithmetic: none -> 2.65 us  [slab_terms(): grad * jnp.exp(cumulative).T[:, :, None]]
    unnamed x71 -> x61, local copies, waits for them, and re-layouts: 7.56 us -> 8.11 us
    reshape x2 -> x1, local copies, waits for them, and re-layouts: 4.38 us -> 4.61 us  [carry_across(): both.reshape(2, count, block, 128).transpose(1, 0, 2, 3)]
  transfers between devices with their start and end apart: 15 -> 15, of which waited for: 9 -> 8; matrix products, arithmetic and copies ran while one was open for 17% -> 17% of each run, Pallas kernels for 0% -> 0%
where the time goes in v1:
time: 228 us; the launch traced here: 227 us
  waiting for transfers between devices  72 us (32%)
  starting transfers between devices  49.9 us (22%)
  matrix products  35.8 us (16%)
  local copies, waits for them, and re-layouts  34 us (15%)
  other arithmetic  33.6 us (15%)
    all_to_all x1, waiting for transfers between devices, carry_across(): lax.all_to_all(back.reshape(count * 2 * block, 128), 'ctx', 0, 0, tiled=T...  41.2 us
    ppermute x12, starting transfers between devices, exchange(): return lax.ppermute(value, axis, [(i, i ^ distance) for i in range(count)])  22.9 us
    all_to_all x1, waiting for transfers between devices, carry_across(): lax.all_to_all(payload.reshape(count * chunk, 128), 'ctx', 0, 0, tiled=True)  20.7 us
    dot_general x2, matrix products, slab_local(): local_part = jnp.einsum('gjqk,kgjp->qgjp', mixed, scaled, precision=fast)  11.2 us
    all_to_all x1, starting transfers between devices, carry_across(): lax.all_to_all(back.reshape(count * 2 * block, 128), 'ctx', 0, 0, tiled=T...  10.7 us
    ppermute x12, waiting for transfers between devices, exchange(): return lax.ppermute(value, axis, [(i, i ^ distance) for i in range(count)])  10.1 us
    all_to_all x1, starting transfers between devices, per_device(): own_totals = jnp.sum(lax.all_to_all(dealt, 'dp', 0, 0, tiled=True), axis=0)  8.98 us
    unnamed x61, local copies, waits for them, and re-layouts  8.11 us
  transfers between devices with their start and end apart: 15, of which 8 were waited for; matrix products, arithmetic and copies ran while one was open for 17% of the time, Pallas kernels for 0%

profile of v1, /device:TPU:2, one launch (start us, length us, event | category | flops | bytes accessed | tf_op | source)
XLA Modules:
  0.0 226.6 jit_solution(18099485835227643783)
XLA Ops:
  2.0 6.6 %collective-permute-start.2 = (f32[3,4]{1,0:T(4,128)}, f32[3,4]{1,0:T(4,128)S(1)}, u32[]{:S(2)}, u32[]{:S(2)}) collective-permute-start(f32[3,4]{1,0:T(4,128)} %pad_maximum_fusion.1), channel_id=1, source_target_pairs={{0,3},{1,2},{2,1},{3,0},{4,7},{5,6},{6,5},{7,4},{8,11},{9,10},{10,... | collective-permute-start | bytes 152 | tf_op jit(solution)/shard_map/ppermute | solution.py:113
  28.4 3.2 %fusion = f32[2,8,8,64,64]{4,3,2,1,0:T(8,128)} fusion(f32[128,8,1,8,64]{0,4,3,1,2:T(8,128)S(1)} %get-tuple-element.146, f32[128,8,1,8,64]{0,4,3,1,2:T(8,128)S(1)} %get-tuple-element.147, bf16[128,8,1,64]{0,3,1,2:T(8,128)(2,1)S(1)} %bitcast.233, bf16[128,8,1,64]{0,3,1,2:T(8,128)(2,1)S(1)} %bitcast.237), kind=kOutput, calls=%fused_computation | convolution fusion | flops 403832832 | bytes 6553600 | tf_op jit(solution)/shard_map/tgwn,tgwjp->wgjpn/dot_general | solution.py:63
  31.6 4.6 %reshape.356 = f32[2,16,128,128]{3,2,1,0:T(8,128)} reshape(f32[2,64,64,64]{3,2,1,0:T(8,128)} %bitcast.224) | data formatting | bytes 4194304 | tf_op jit(solution)/shard_map/reshape | solution.py:78
  36.2 3.1 %copy.154 = f32[16,2,128,128]{3,2,1,0:T(8,128)} copy(f32[16,2,128,128]{3,2,0,1:T(8,128)} %bitcast.225) | data formatting | bytes 4194304 | tf_op jit(solution)/shard_map/transpose | solution.py:78
  39.5 3.2 %maximum_maximum_fusion = f32[16,264,128]{2,1,0:T(8,128)} fusion(f32[16,4,128]{2,1,0:T(4,128)S(1)} %broadcast_in_dim.46, f32[16,256,128]{2,1,0:T(8,128)} %bitcast.226, f32[264]{0:T(512)S(1)} %pad.15.clone), kind=kLoop, calls=%fused_computation.12 | loop fusion | flops 1081344 | bytes 4293664 | tf_op jit(solution)/shard_map/concatenate | solution.py:83
  42.7 7.3 %all-to-all-start = ((f32[16,264,128]{2,1,0:T(8,128)}), f32[16,264,128]{2,1,0:T(8,128)}, u32[]{:S(2)}, u32[]{:S(2)}) async-start(f32[16,264,128]{2,1,0:T(8,128)} %maximum_maximum_fusion), calls=%async_computation | async-start | bytes 4325376 | tf_op jit(solution)/shard_map/all_to_all | solution.py:85
  53.1 4.7 %fusion.4 = f32[8,8,64,128]{3,2,1,0:T(8,128)S(1)} fusion(f32[8,8,64,128]{3,2,1,0:T(8,128)} %bitcast.219, f32[8,128,128]{2,1,0:T(8,128)S(1)} %fusion.79, f32[8,8,128]{2,1,0:T(8,128)S(1)} %reduce_window_sum.45, pred[128,128]{1,0:T(8,128)(4,1)S(1)} %iota_compare_fusion), kind=kOutput, calls=%fused_computation.6 | convolution fusion | flops 406847488 | bytes 4767744 | tf_op jit(solution)/shard_map/transpose(jvp(gjqk,kgjp->qgjp))/dot_general | solution.py:34
  60.3 6.5 %fusion.9 = (f32[8,8,128]{2,1,0:T(8,128)S(1)}, f32[8,8,128]{2,1,0:T(8,128)S(1)}, f32[8,128,128]{2,1,0:T(8,128)S(1)}) fusion(f32[8,128,128]{2,1,0:T(8,128)S(1)} %fusion.79, f32[8,8,128]{2,1,0:T(8,128)S(1)} %reduce_window_sum.45, pred[128,128]{1,0:T(8,128)(4,1)S(1)} %iota_compare_fusion, f32[8,8,64,128]{3,2,1,0:T(8,128)S(1)} %bitcast.223, ...), kind=kOutput, calls=%fused_computation.11 | convolution fusion | flops 414040064 | bytes 5357568 | tf_op jit(solution)/shard_map/transpose(jvp(gjqk,kgjp->qgjp))/dot_general | solution.py:34
  72.4 20.7 %all-to-all-done = f32[16,264,128]{2,1,0:T(8,128)} async-done(((f32[16,264,128]{2,1,0:T(8,128)}), f32[16,264,128]{2,1,0:T(8,128)}, u32[]{:S(2)}, u32[]{:S(2)}) %all-to-all-start) | async-done | bytes 2162720 | tf_op jit(solution)/shard_map/all_to_all | solution.py:85
  93.9 3.1 %fusion.78 = (f32[16,128,128]{2,1,0:T(8,128)}, f32[16,128,128]{2,1,0:T(8,128)}) fusion(f32[16,264,128]{2,1,0:T(8,128)} %bitcast.38), kind=kLoop, calls=%fused_computation.143 | loop fusion | bytes 4194304 | tf_op jit(solution)/shard_map/slice | solution.py:88
  104.8 10.7 %all-to-all-start.1 = ((f32[16,256,128]{2,1,0:T(8,128)}), f32[16,256,128]{2,1,0:T(8,128)}, u32[]{:S(2)}, u32[]{:S(2)}) async-start(f32[16,256,128]{2,1,0:T(8,128)} %pad_maximum_fusion), calls=%async_computation.1 | async-start | bytes 4194304 | tf_op jit(solution)/shard_map/all_to_all | solution.py:104
  116.4 41.2 %all-to-all-done.1 = f32[16,256,128]{2,1,0:T(8,128)} async-done(((f32[16,256,128]{2,1,0:T(8,128)}), f32[16,256,128]{2,1,0:T(8,128)}, u32[]{:S(2)}, u32[]{:S(2)}) %all-to-all-start.1) | async-done | bytes 2097184 | tf_op jit(solution)/shard_map/all_to_all | solution.py:104
  157.7 3.2 %slice_multiply_fusion = (f32[16,128,128]{2,1,0:T(8,128)}, f32[16,128,128]{2,1,0:T(8,128)}, f32[16,128,128]{2,1,0:T(8,128)S(1)}) fusion(f32[16,256,128]{2,1,0:T(8,128)} %all-to-all-done.1), kind=kLoop, calls=%fused_computation.138 | loop fusion | flops 262144 | bytes 5242880 | tf_op jit(solution)/shard_map/transpose(jvp())/mul | solution.py:46
  160.9 2.7 %mul.296 = f32[64,64,64]{2,1,0:T(8,128)} reshape(f32[16,128,128]{2,1,0:T(8,128)} %get-tuple-element.115) | data formatting | bytes 2097152 | tf_op jit(solution)/shard_map/transpose(jvp())/mul | solution.py:46
  163.6 2.7 %reduce_sum.167 = f32[64]{0:T(128)} reduce(f32[64,64,64]{2,1,0:T(8,128)} %mul.296, f32[]{:T(128)} %constant.91.clone.1), dimensions={1,2}, to_apply=%region_14.16 | reduce | flops 262080 | bytes 1048836 | tf_op jit(solution)/shard_map/transpose(jvp())/reduce_sum | solution.py:46
  170.5 2.7 %reshape_reshape.8 = f32[8,8,64,64]{3,2,1,0:T(8,128)} reshape(f32[16,128,128]{2,1,0:T(8,128)} %get-tuple-element.116) | data formatting | bytes 2097152 | tf_op jit(solution)/shard_map/jvp()/reshape;reshape | solution.py:47
  173.3 3.6 %fusion.12 = f32[128,8,8]{0,2,1:T(8,128)} fusion(f32[128,8,8,64]{0,3,2,1:T(8,128)} %bitcast.220, f32[8,8,64,64]{3,2,1,0:T(8,128)} %reshape_reshape.8, bf16[128,8,64,1]{0,2,3,1:T(8,128)(2,1)S(1)} %bitcast.234), kind=kOutput, calls=%fused_computation.18 | convolution fusion | flops 202366976 | bytes 3309568 | tf_op jit(solution)/shard_map/jvp(qgn,gjpn->qgjp)/dot_general | solution.py:48
  179.5 4.3 %fusion.17 = (f32[128,8,8]{0,2,1:T(8,128)S(1)}, f32[8,8,64,128]{3,2,1,0:T(8,128)}) fusion(f32[128,8,8,64]{0,3,2,1:T(8,128)S(1)} %bitcast.216, f32[8,8,64,64]{3,2,1,0:T(8,128)} %reshape_reshape.7, f32[128,8,8]{0,2,1:T(8,128)S(1)} %bitcast.242, f32[128,8,64]{0,2,1:T(8,128)S(1)} %convert.10), kind=kOutput, calls=%fused_computation.26 | convolution fusion | flops 202891264 | bytes 5570560 | tf_op jit(solution)/shard_map/transpose(jvp(kgjn,kgjp->gjpn))/dot_general | solution.py:44
  189.2 9.0 %all-to-all-start.2 = ((f32[16,3,4]{2,1,0:T(4,128)}), f32[16,3,4]{2,1,0:T(4,128)S(1)}, u32[]{:S(2)}, u32[]{:S(2)}) async-start(f32[16,3,4]{2,1,0:T(4,128)} %copy.171), calls=%async_computation.2 | async-start | bytes 65536 | tf_op jit(solution)/shard_map/all_to_all | solution.py:175
  198.3 4.3 %fusion.36 = bf16[128,8,64]{0,2,1:T(8,128)(2,1)S(1)} fusion(f32[128,8,64]{0,2,1:T(8,128)S(1)} %copy-done.10, f32[8,8,64,64]{3,2,1,0:T(8,128)} %reshape_reshape.8, f32[128,8,8,64]{0,3,2,1:T(8,128)} %bitcast.221, f32[128,8,8]{0,2,1:T(8,128)S(1)} %bitcast.244), kind=kOutput, calls=%fused_computation.46 | convolution fusion | flops 201981952 | bytes 3571712 | tf_op jit(solution)/shard_map/transpose(jvp(qgn,gjpn->qgjp))/dot_general | solution.py:48
  206.9 3.7 %collective-permute-start.8 = (f32[3,4]{1,0:T(4,128)S(1)}, f32[3,4]{1,0:T(4,128)S(1)}, u32[]{:S(2)}, u32[]{:S(2)}) collective-permute-start(f32[3,4]{1,0:T(4,128)S(1)} %reduce_sum.176), channel_id=1, source_target_pairs={{0,48},{16,32},{32,16},{48,0},{64,112},{80,96},{96,80},{112,64},{1... | collective-permute-start | bytes 152 | tf_op jit(solution)/shard_map/ppermute | solution.py:113
  212.2 3.5 %collective-permute-done.7 = f32[3,4]{1,0:T(4,128)S(1)} collective-permute-done((f32[3,4]{1,0:T(4,128)S(1)}, f32[3,4]{1,0:T(4,128)S(1)}, u32[]{:S(2)}, u32[]{:S(2)}) %collective-permute-start.7) | collective-permute-done | bytes 80 | tf_op jit(solution)/shard_map/ppermute | solution.py:113
  215.7 5.8 %collective-permute-start.11 = (f32[3,4]{1,0:T(4,128)S(1)}, f32[3,4]{1,0:T(4,128)S(1)}, u32[]{:S(2)}, u32[]{:S(2)}) collective-permute-start(f32[3,4]{1,0:T(4,128)S(1)} %add_add_fusion.1), channel_id=1, source_target_pairs={{0,192},{16,208},{32,224},{48,240},{64,128},{80,144},{96,160},{112... | collective-permute-start | bytes 152 | tf_op jit(solution)/shard_map/ppermute | solution.py:113
  223.1 2.9 %collective-permute-done.10 = f32[3,4]{1,0:T(4,128)S(1)} collective-permute-done((f32[3,4]{1,0:T(4,128)S(1)}, f32[3,4]{1,0:T(4,128)S(1)}, u32[]{:S(2)}, u32[]{:S(2)}) %collective-permute-start.10) | collective-permute-done | bytes 80 | tf_op jit(solution)/shard_map/ppermute | solution.py:113
  (155 shorter events, 61.7 us)
Async XLA Ops:
  0.6 12.1 %copy-start.9 = (bf16[1,128,4096]{2,1,0:T(8,128)(2,1)S(1)}, bf16[1,128,4096]{2,1,0:T(8,128)(2,1)}, u32[]{:S(2)}) copy-start(bf16[1,128,4096]{2,1,0:T(8,128)(2,1)} %param.9) | copy-start | bytes 3145732
  2.0 14.7 %collective-permute-start.2 = (f32[3,4]{1,0:T(4,128)}, f32[3,4]{1,0:T(4,128)S(1)}, u32[]{:S(2)}, u32[]{:S(2)}) collective-permute-start(f32[3,4]{1,0:T(4,128)} %pad_maximum_fusion.1), channel_id=1, source_target_pairs={{0,3},{1,2},{2,1},{3,0},{4,7},{5,6},{6,5},{7,4},{8,11},{9,10},{10,... | collective-permute-start | bytes 152 | tf_op jit(solution)/shard_map/ppermute | solution.py:113
  8.6 8.1 %collective-permute-start.1 = (f32[3,4]{1,0:T(4,128)}, f32[3,4]{1,0:T(4,128)S(1)}, u32[]{:S(2)}, u32[]{:S(2)}) collective-permute-start(f32[3,4]{1,0:T(4,128)} %pad_maximum_fusion.1), channel_id=1, source_target_pairs={{0,2},{1,3},{2,0},{3,1},{4,6},{5,7},{6,4},{7,5},{8,10},{9,11},{10,... | collective-permute-start | bytes 152 | tf_op jit(solution)/shard_map/ppermute | solution.py:113
  9.2 7.5 %collective-permute-start = (f32[3,4]{1,0:T(4,128)}, f32[3,4]{1,0:T(4,128)S(1)}, u32[]{:S(2)}, u32[]{:S(2)}) collective-permute-start(f32[3,4]{1,0:T(4,128)} %pad_maximum_fusion.1), channel_id=1, source_target_pairs={{0,1},{1,0},{2,3},{3,2},{4,5},{5,4},{6,7},{7,6},{8,9},{9,8},{10,11... | collective-permute-start | bytes 152 | tf_op jit(solution)/shard_map/ppermute | solution.py:113
  15.2 8.4 %copy-start.12 = (f32[1,64,128]{2,1,0:T(8,128)S(1)}, f32[1,64,128]{2,1,0:T(8,128)}, u32[]{:S(2)}) copy-start(f32[1,64,128]{2,1,0:T(8,128)} %param.12) | copy-start | bytes 98308
  16.9 4.2 %collective-permute-start.5 = (f32[3,16]{1,0:T(4,128)S(1)}, f32[3,16]{1,0:T(4,128)S(1)}, u32[]{:S(2)}, u32[]{:S(2)}) collective-permute-start(f32[3,16]{1,0:T(4,128)S(1)} %pad_maximum_fusion.2), channel_id=1, source_target_pairs={{0,12},{1,13},{2,14},{3,15},{4,8},{5,9},{6,10},{7,11},{8,4},{9,5},... | collective-permute-start | bytes 584 | tf_op jit(solution)/shard_map/ppermute | solution.py:113
  18.4 5.1 %collective-permute-start.4 = (f32[3,16]{1,0:T(4,128)S(1)}, f32[3,16]{1,0:T(4,128)S(1)}, u32[]{:S(2)}, u32[]{:S(2)}) collective-permute-start(f32[3,16]{1,0:T(4,128)S(1)} %pad_maximum_fusion.2), channel_id=1, source_target_pairs={{0,8},{1,9},{2,10},{3,11},{4,12},{5,13},{6,14},{7,15},{8,0},{9,1},... | collective-permute-start | bytes 584 | tf_op jit(solution)/shard_map/ppermute | solution.py:113
  19.7 3.8 %collective-permute-start.3 = (f32[3,16]{1,0:T(4,128)S(1)}, f32[3,16]{1,0:T(4,128)S(1)}, u32[]{:S(2)}, u32[]{:S(2)}) collective-permute-start(f32[3,16]{1,0:T(4,128)S(1)} %pad_maximum_fusion.2), channel_id=1, source_target_pairs={{0,4},{1,5},{2,6},{3,7},{4,0},{5,1},{6,2},{7,3},{8,12},{9,13},{10,... | collective-permute-start | bytes 584 | tf_op jit(solution)/shard_map/ppermute | solution.py:113
  23.6 4.8 %copy-start.18 = (f32[3,64]{1,0:T(4,128)}, f32[3,64]{1,0:T(4,128)S(1)}, u32[]{:S(2)}) copy-start(f32[3,64]{1,0:T(4,128)S(1)} %pad_maximum_fusion.3) | copy-start | bytes 2308
  23.6 4.8 %copy-start.23 = (f32[64]{0:T(128)}, f32[64]{0:T(128)S(1)}, u32[]{:S(2)}) copy-start(f32[64]{0:T(128)S(1)} %exponential_negate_fusion.1) | copy-start | bytes 772
  42.7 7.4 %copy-start.13 = (f32[1,64,128]{2,1,0:T(8,128)S(1)}, f32[1,64,128]{2,1,0:T(8,128)}, u32[]{:S(2)}) copy-start(f32[1,64,128]{2,1,0:T(8,128)} %param.12) | copy-start | bytes 98308
  42.7 9.7 %copy-start.5 = (f32[128,8,64]{0,2,1:T(8,128)S(1)}, f32[128,8,64]{0,2,1:T(8,128)}, u32[]{:S(2)}) copy-start(f32[128,8,64]{0,2,1:T(8,128)} %convert_element_type.140) | copy-start | bytes 786436
  42.7 50.3 %all-to-all-start = ((f32[16,264,128]{2,1,0:T(8,128)}), f32[16,264,128]{2,1,0:T(8,128)}, u32[]{:S(2)}, u32[]{:S(2)}) async-start(f32[16,264,128]{2,1,0:T(8,128)} %maximum_maximum_fusion), calls=%async_computation | async-start | bytes 4325376 | tf_op jit(solution)/shard_map/all_to_all | solution.py:85
  53.1 4.7 %copy-start = (f32[1,128,4096]{1,2,0:T(8,128)S(1)}, f32[1,128,4096]{1,2,0:T(8,128)}, u32[]{:S(2)}) copy-start(f32[1,128,4096]{1,2,0:T(8,128)} %convert_element_type.155) | copy-start | bytes 6291460
  104.8 52.9 %all-to-all-start.1 = ((f32[16,256,128]{2,1,0:T(8,128)}), f32[16,256,128]{2,1,0:T(8,128)}, u32[]{:S(2)}, u32[]{:S(2)}) async-start(f32[16,256,128]{2,1,0:T(8,128)} %pad_maximum_fusion), calls=%async_computation.1 | async-start | bytes 4194304 | tf_op jit(solution)/shard_map/all_to_all | solution.py:104
  183.9 14.3 %copy-start.11 = (f32[128,8,64]{0,2,1:T(8,128)S(1)}, f32[128,8,64]{0,2,1:T(8,128)}, u32[]{:S(2)}) copy-start(f32[128,8,64]{0,2,1:T(8,128)} %convolution_bitcast_fusion.1) | copy-start | bytes 786436
  183.9 14.3 %copy-start.10 = (f32[128,8,64]{0,2,1:T(8,128)S(1)}, f32[128,8,64]{0,2,1:T(8,128)}, u32[]{:S(2)}) copy-start(f32[128,8,64]{0,2,1:T(8,128)} %convolution_bitcast_fusion) | copy-start | bytes 786436
  189.2 17.7 %all-to-all-start.2 = ((f32[16,3,4]{2,1,0:T(4,128)}), f32[16,3,4]{2,1,0:T(4,128)S(1)}, u32[]{:S(2)}, u32[]{:S(2)}) async-start(f32[16,3,4]{2,1,0:T(4,128)} %copy.171), calls=%async_computation.2 | async-start | bytes 65536 | tf_op jit(solution)/shard_map/all_to_all | solution.py:175
  206.9 5.3 %collective-permute-start.8 = (f32[3,4]{1,0:T(4,128)S(1)}, f32[3,4]{1,0:T(4,128)S(1)}, u32[]{:S(2)}, u32[]{:S(2)}) collective-permute-start(f32[3,4]{1,0:T(4,128)S(1)} %reduce_sum.176), channel_id=1, source_target_pairs={{0,48},{16,32},{32,16},{48,0},{64,112},{80,96},{96,80},{112,64},{1... | collective-permute-start | bytes 152 | tf_op jit(solution)/shard_map/ppermute | solution.py:113
  210.6 5.1 %collective-permute-start.7 = (f32[3,4]{1,0:T(4,128)S(1)}, f32[3,4]{1,0:T(4,128)S(1)}, u32[]{:S(2)}, u32[]{:S(2)}) collective-permute-start(f32[3,4]{1,0:T(4,128)S(1)} %reduce_sum.176), channel_id=1, source_target_pairs={{0,32},{16,48},{32,0},{48,16},{64,96},{80,112},{96,64},{112,80},{1... | collective-permute-start | bytes 152 | tf_op jit(solution)/shard_map/ppermute | solution.py:113
  211.3 4.4 %collective-permute-start.6 = (f32[3,4]{1,0:T(4,128)S(1)}, f32[3,4]{1,0:T(4,128)S(1)}, u32[]{:S(2)}, u32[]{:S(2)}) collective-permute-start(f32[3,4]{1,0:T(4,128)S(1)} %reduce_sum.176), channel_id=1, source_target_pairs={{0,16},{16,0},{32,48},{48,32},{64,80},{80,64},{96,112},{112,96},{1... | collective-permute-start | bytes 152 | tf_op jit(solution)/shard_map/ppermute | solution.py:113
  215.7 7.4 %collective-permute-start.11 = (f32[3,4]{1,0:T(4,128)S(1)}, f32[3,4]{1,0:T(4,128)S(1)}, u32[]{:S(2)}, u32[]{:S(2)}) collective-permute-start(f32[3,4]{1,0:T(4,128)S(1)} %add_add_fusion.1), channel_id=1, source_target_pairs={{0,192},{16,208},{32,224},{48,240},{64,128},{80,144},{96,160},{112... | collective-permute-start | bytes 152 | tf_op jit(solution)/shard_map/ppermute | solution.py:113
  221.5 4.5 %collective-permute-start.10 = (f32[3,4]{1,0:T(4,128)S(1)}, f32[3,4]{1,0:T(4,128)S(1)}, u32[]{:S(2)}, u32[]{:S(2)}) collective-permute-start(f32[3,4]{1,0:T(4,128)S(1)} %add_add_fusion.1), channel_id=1, source_target_pairs={{0,128},{16,144},{32,160},{48,176},{64,192},{80,208},{96,224},{112... | collective-permute-start | bytes 152 | tf_op jit(solution)/shard_map/ppermute | solution.py:113
  222.5 3.6 %collective-permute-start.9 = (f32[3,4]{1,0:T(4,128)S(1)}, f32[3,4]{1,0:T(4,128)S(1)}, u32[]{:S(2)}, u32[]{:S(2)}) collective-permute-start(f32[3,4]{1,0:T(4,128)S(1)} %add_add_fusion.1), channel_id=1, source_target_pairs={{0,64},{16,80},{32,96},{48,112},{64,0},{80,16},{96,32},{112,48},{1... | collective-permute-start | bytes 152 | tf_op jit(solution)/shard_map/ppermute | solution.py:113
  (18 other events, 52.3 us)

commit v2 on v0

--- a/solution.py
+++ b/solution.py
@@ -12,11 +12,18 @@
 fast = lax.Precision.HIGH
 
 
+def running_sum(values):
+    tokens = values.shape[-1]
+    offsets = jnp.arange(tokens)
+    upper = (offsets[:, None] <= offsets[None, :]).astype(values.dtype)
+    return jnp.einsum("ht,ts->hs", values, upper, precision=highest)
+
+
 def slab_prelude(x, raw, bias, alog):
     tokens, num_heads, width = x.shape
     dt_value = jax.nn.softplus(raw + bias[:, None])
     log_decay = dt_value * (-jnp.exp(alog))[:, None]
-    cumulative = jnp.cumsum(log_decay, axis=1)
+    cumulative = running_sum(log_decay)
     scaled = (x * dt_value.T[:, :, None]).reshape(tokens, G, num_heads // G, width)
     return cumulative, scaled
 
@@ -55,7 +62,7 @@
     group_heads = num_heads // G
     dt_value = jax.nn.softplus(raw + bias[:, None])
     log_decay = dt_value * (-jnp.exp(alog))[:, None]
-    cumulative = jnp.cumsum(log_decay, axis=1)
+    cumulative = running_sum(log_decay)
     total = cumulative[:, -1]
     tail_decay = jnp.exp(total[:, None] - cumulative)
     carried = (x * (dt_value * tail_decay).T[:, :, None]).reshape(tokens, G, group_heads, width)

time: 225 us -> 221 us (0.982)
  other arithmetic: 30.5 us -> 21 us
  waiting for transfers between devices: 72.2 us -> 76.4 us
  matrix products: 38.6 us -> 41.3 us
    another operation x4 -> x0, other arithmetic: 5.07 us -> none  [the longest x3 4.79 us: slab_prelude(): cumulative = jnp.cumsum(log_decay, axis=1)]
    dot_general x0 -> x5, matrix products: none -> 3.79 us  [running_sum(): return jnp.einsum('ht,ts->hs', values, upper, precision=highest)]
    all_to_all x1, waiting for transfers between devices: 20.7 us -> 23.8 us  [carry_across(): lax.all_to_all(payload.reshape(count * chunk, 128), 'ctx', 0, 0, tiled=True)]
    unnamed x71 -> x79, local copies, waits for them, and re-layouts: 7.56 us -> 8.16 us
  transfers between devices with their start and end apart: 15 -> 15, of which waited for: 9 -> 9; matrix products, arithmetic and copies ran while one was open for 17% -> 15% of each run, Pallas kernels for 0% -> 0%
where the time goes in v2:
time: 221 us; the launch traced here: 220 us
  waiting for transfers between devices  76.4 us (35%)
  starting transfers between devices  49 us (22%)
  matrix products  41.3 us (19%)
  local copies, waits for them, and re-layouts  30.9 us (14%)
  other arithmetic  21 us (10%)
    all_to_all x1, waiting for transfers between devices, carry_across(): lax.all_to_all(back.reshape(count * 2 * block, 128), 'ctx', 0, 0, tiled=T...  41 us
    all_to_all x1, waiting for transfers between devices, carry_across(): lax.all_to_all(payload.reshape(count * chunk, 128), 'ctx', 0, 0, tiled=True)  23.8 us
    ppermute x12, starting transfers between devices, exchange(): return lax.ppermute(value, axis, [(i, i ^ distance) for i in range(count)])  22.8 us
    ppermute x12, waiting for transfers between devices, exchange(): return lax.ppermute(value, axis, [(i, i ^ distance) for i in range(count)])  11.6 us
    dot_general x2, matrix products, slab_local(): local_part = jnp.einsum('gjqk,kgjp->qgjp', mixed, scaled, precision=fast)  11.2 us
    all_to_all x1, starting transfers between devices, carry_across(): lax.all_to_all(back.reshape(count * 2 * block, 128), 'ctx', 0, 0, tiled=T...  10.9 us
    all_to_all x1, starting transfers between devices, per_device(): own_totals = jnp.sum(lax.all_to_all(dealt, 'dp', 0, 0, tiled=True), axis=0)  8.99 us
    unnamed x79, local copies, waits for them, and re-layouts  8.16 us
  transfers between devices with their start and end apart: 15, of which 9 were waited for; matrix products, arithmetic and copies ran while one was open for 15% of the time, Pallas kernels for 0%

profile of v2, /device:TPU:2, one launch (start us, length us, event | category | flops | bytes accessed | tf_op | source)
XLA Modules:
  0.0 220.1 jit_solution(1548755476229336357)
XLA Ops:
  2.0 6.6 %collective-permute-start.2 = (f32[3,4]{1,0:T(4,128)}, f32[3,4]{1,0:T(4,128)S(1)}, u32[]{:S(2)}, u32[]{:S(2)}) collective-permute-start(f32[3,4]{1,0:T(4,128)} %pad_maximum_fusion.1), channel_id=1, source_target_pairs={{0,3},{1,2},{2,1},{3,0},{4,7},{5,6},{6,5},{7,4},{8,11},{9,10},{10,... | collective-permute-start | bytes 152 | tf_op jit(solution)/shard_map/ppermute | solution.py:121
  31.6 2.6 %reshape.315 = f32[16,128,128]{2,1,0:T(8,128)} reshape(f32[64,64,64]{2,1,0:T(8,128)} %bitcast.230) | data formatting | bytes 2097152 | tf_op jit(solution)/shard_map/reshape | solution.py:86
  34.3 2.8 %maximum_maximum_fusion = f32[16,264,128]{2,1,0:T(8,128)} fusion(f32[16,4,128]{2,1,0:T(4,128)S(1)} %broadcast_in_dim.46, f32[16,128,128]{2,1,0:T(8,128)} %reshape.315, f32[16,128,128]{2,1,0:T(8,128)S(1)} %reshape.314, f32[264]{0:T(512)S(1)} %pad.16.clone), kind=kLoop, calls=%fused_computation.8 | loop fusion | flops 1622016 | bytes 4293664 | tf_op jit(solution)/shard_map/concatenate | solution.py:91
  37.1 6.2 %all-to-all-start = ((f32[16,264,128]{2,1,0:T(8,128)}), f32[16,264,128]{2,1,0:T(8,128)}, u32[]{:S(2)}, u32[]{:S(2)}) async-start(f32[16,264,128]{2,1,0:T(8,128)} %maximum_maximum_fusion), calls=%async_computation | async-start | bytes 4325376 | tf_op jit(solution)/shard_map/all_to_all | solution.py:93
  44.5 4.7 %fusion = f32[8,8,64,128]{3,2,1,0:T(8,128)S(1)} fusion(f32[8,8,64,128]{3,2,1,0:T(8,128)} %bitcast.225, f32[8,128,128]{2,1,0:T(8,128)S(1)} %fusion.99, f32[8,8,128]{2,1,0:T(8,128)S(1)} %convolution_bitcast_fusion.2, pred[128,128]{1,0:T(8,128)(4,1)S(1)} %iota_compare_fusion), kind=kOutput, calls=%fused_computation.2 | convolution fusion | flops 406847488 | bytes 4767744 | tf_op jit(solution)/shard_map/transpose(jvp(gjqk,kgjp->qgjp))/dot_general | solution.py:41
  49.1 2.5 %multiply_reduce_fusion.1 = (f32[64]{0:T(128)S(1)}, f32[128,64]{0,1:T(8,128)S(1)}, f32[128,64,64]{0,2,1:T(8,128)}, f32[128,64,64]{0,2,1:T(8,128)S(1)}) fusion(f32[128,64,64]{0,2,1:T(8,128)S(1)} %bitcast.228, f32[128,64,64]{0,2,1:T(8,128)S(1)} %bitcast.221, f32[8,8,64,128]{3,2,1,0:T(8,128)S(1)} %fusion, f32[128,64]{0,1:T(8,128)S(1)} %fusion.89, ...), kind=kLoop, calls=%fused_computation.32 | loop fusion | flops 4186048 | bytes 10551808 | tf_op jit(solution)/shard_map/transpose(jvp())/reduce_sum | solution.py:42
  51.7 6.5 %fusion.5 = (f32[8,8,128]{2,1,0:T(8,128)S(1)}, f32[8,8,128]{2,1,0:T(8,128)S(1)}, f32[8,128,128]{2,1,0:T(8,128)S(1)}) fusion(f32[8,128,128]{2,1,0:T(8,128)S(1)} %fusion.99, f32[8,8,128]{2,1,0:T(8,128)S(1)} %convolution_bitcast_fusion.2, pred[128,128]{1,0:T(8,128)(4,1)S(1)} %iota_compare_fusion, f32[8,8,64,128]{3,2,1,0:T(8,128)S(1)} %bitcast.229, ...), kind=kOutput, calls=%fused_computation.7 | convolution fusion | flops 414040064 | bytes 5357568 | tf_op jit(solution)/shard_map/transpose(jvp(gjqk,kgjp->qgjp))/dot_general | solution.py:41
  62.6 23.8 %all-to-all-done = f32[16,264,128]{2,1,0:T(8,128)} async-done(((f32[16,264,128]{2,1,0:T(8,128)}), f32[16,264,128]{2,1,0:T(8,128)}, u32[]{:S(2)}, u32[]{:S(2)}) %all-to-all-start) | async-done | bytes 2162720 | tf_op jit(solution)/shard_map/all_to_all | solution.py:93
  87.2 3.1 %fusion.96 = (f32[16,128,128]{2,1,0:T(8,128)}, f32[16,128,128]{2,1,0:T(8,128)}) fusion(f32[16,264,128]{2,1,0:T(8,128)} %bitcast.37), kind=kLoop, calls=%fused_computation.156 | loop fusion | bytes 4194304 | tf_op jit(solution)/shard_map/slice | solution.py:96
  91.7 2.9 %fusion.44 = f32[64,32,128]{2,0,1:T(8,128)S(1)} fusion(f32[64,64,1]{1,0,2:T(8,128)S(1)} %reshape.335, f32[64,32,128]{2,1,0:T(8,128)} %bitcast.234), kind=kOutput, calls=%fused_computation.54 | convolution fusion | flops 201326592 | bytes 2113536 | tf_op jit(solution)/shard_map/ab,brl->arl/dot_general | solution.py:107
  99.0 10.9 %all-to-all-start.1 = ((f32[16,256,128]{2,1,0:T(8,128)}), f32[16,256,128]{2,1,0:T(8,128)}, u32[]{:S(2)}, u32[]{:S(2)}) async-start(f32[16,256,128]{2,1,0:T(8,128)} %pad_maximum_fusion), calls=%async_computation.1 | async-start | bytes 4194304 | tf_op jit(solution)/shard_map/all_to_all | solution.py:112
  111.0 41.0 %all-to-all-done.1 = f32[16,256,128]{2,1,0:T(8,128)} async-done(((f32[16,256,128]{2,1,0:T(8,128)}), f32[16,256,128]{2,1,0:T(8,128)}, u32[]{:S(2)}, u32[]{:S(2)}) %all-to-all-start.1) | async-done | bytes 2097184 | tf_op jit(solution)/shard_map/all_to_all | solution.py:112
  152.0 3.2 %slice_multiply_fusion = (f32[16,128,128]{2,1,0:T(8,128)}, f32[16,128,128]{2,1,0:T(8,128)}, f32[16,128,128]{2,1,0:T(8,128)S(1)}) fusion(f32[16,256,128]{2,1,0:T(8,128)} %all-to-all-done.1), kind=kLoop, calls=%fused_computation.151 | loop fusion | flops 262144 | bytes 5242880 | tf_op jit(solution)/shard_map/transpose(jvp())/mul | solution.py:53
  155.3 2.7 %mul.284 = f32[64,64,64]{2,1,0:T(8,128)} reshape(f32[16,128,128]{2,1,0:T(8,128)} %get-tuple-element.110) | data formatting | bytes 2097152 | tf_op jit(solution)/shard_map/transpose(jvp())/mul | solution.py:53
  158.0 2.7 %reduce_sum.167 = f32[64]{0:T(128)} reduce(f32[64,64,64]{2,1,0:T(8,128)} %mul.284, f32[]{:T(128)} %constant.81.clone.1), dimensions={1,2}, to_apply=%region_10.12 | reduce | flops 262080 | bytes 1048836 | tf_op jit(solution)/shard_map/transpose(jvp())/reduce_sum | solution.py:53
  165.4 2.7 %reshape_reshape.8 = f32[8,8,64,64]{3,2,1,0:T(8,128)} reshape(f32[16,128,128]{2,1,0:T(8,128)} %get-tuple-element.111) | data formatting | bytes 2097152 | tf_op jit(solution)/shard_map/jvp()/reshape;reshape | solution.py:54
  168.1 3.6 %fusion.8 = f32[128,8,8]{0,2,1:T(8,128)} fusion(f32[128,8,8,64]{0,3,2,1:T(8,128)} %bitcast.226, f32[8,8,64,64]{3,2,1,0:T(8,128)} %reshape_reshape.8, bf16[128,8,64,1]{0,2,3,1:T(8,128)(2,1)S(1)} %bitcast.239), kind=kOutput, calls=%fused_computation.14 | convolution fusion | flops 202366976 | bytes 3309568 | tf_op jit(solution)/shard_map/jvp(qgn,gjpn->qgjp)/dot_general | solution.py:55
  174.3 4.3 %fusion.13 = (f32[128,8,8]{0,2,1:T(8,128)S(1)}, f32[8,8,64,128]{3,2,1,0:T(8,128)}) fusion(f32[128,8,8,64]{0,3,2,1:T(8,128)S(1)} %bitcast.222, f32[8,8,64,64]{3,2,1,0:T(8,128)} %reshape_reshape.7, f32[128,8,8]{0,2,1:T(8,128)S(1)} %bitcast.245, f32[128,8,64]{0,2,1:T(8,128)S(1)} %convert_element_type.97), kind=kOutput, calls=%fused_computation.22 | convolution fusion | flops 202891264 | bytes 5570560 | tf_op jit(solution)/shard_map/transpose(jvp(kgjn,kgjp->gjpn))/dot_general | solution.py:51
  182.7 9.0 %all-to-all-start.2 = ((f32[16,3,4]{2,1,0:T(4,128)}), f32[16,3,4]{2,1,0:T(4,128)S(1)}, u32[]{:S(2)}, u32[]{:S(2)}) async-start(f32[16,3,4]{2,1,0:T(4,128)} %copy.131), calls=%async_computation.2 | async-start | bytes 65536 | tf_op jit(solution)/shard_map/all_to_all | solution.py:183
  191.8 4.3 %fusion.36 = bf16[128,8,64]{0,2,1:T(8,128)(2,1)S(1)} fusion(f32[128,8,64]{0,2,1:T(8,128)S(1)} %copy-done.10, f32[8,8,64,64]{3,2,1,0:T(8,128)} %reshape_reshape.8, f32[128,8,8,64]{0,3,2,1:T(8,128)} %bitcast.227, f32[128,8,8]{0,2,1:T(8,128)S(1)} %bitcast.247), kind=kOutput, calls=%fused_computation.46 | convolution fusion | flops 201981952 | bytes 3571712 | tf_op jit(solution)/shard_map/transpose(jvp(qgn,gjpn->qgjp))/dot_general | solution.py:55
  200.4 3.7 %collective-permute-start.8 = (f32[3,4]{1,0:T(4,128)S(1)}, f32[3,4]{1,0:T(4,128)S(1)}, u32[]{:S(2)}, u32[]{:S(2)}) collective-permute-start(f32[3,4]{1,0:T(4,128)S(1)} %reduce_sum.176), channel_id=1, source_target_pairs={{0,48},{16,32},{32,16},{48,0},{64,112},{80,96},{96,80},{112,64},{1... | collective-permute-start | bytes 152 | tf_op jit(solution)/shard_map/ppermute | solution.py:121
  205.7 3.5 %collective-permute-done.7 = f32[3,4]{1,0:T(4,128)S(1)} collective-permute-done((f32[3,4]{1,0:T(4,128)S(1)}, f32[3,4]{1,0:T(4,128)S(1)}, u32[]{:S(2)}, u32[]{:S(2)}) %collective-permute-start.7) | collective-permute-done | bytes 80 | tf_op jit(solution)/shard_map/ppermute | solution.py:121
  209.2 5.8 %collective-permute-start.11 = (f32[3,4]{1,0:T(4,128)S(1)}, f32[3,4]{1,0:T(4,128)S(1)}, u32[]{:S(2)}, u32[]{:S(2)}) collective-permute-start(f32[3,4]{1,0:T(4,128)S(1)} %add_add_fusion.1), channel_id=1, source_target_pairs={{0,192},{16,208},{32,224},{48,240},{64,128},{80,144},{96,160},{112... | collective-permute-start | bytes 152 | tf_op jit(solution)/shard_map/ppermute | solution.py:121
  216.6 2.9 %collective-permute-done.10 = f32[3,4]{1,0:T(4,128)S(1)} collective-permute-done((f32[3,4]{1,0:T(4,128)S(1)}, f32[3,4]{1,0:T(4,128)S(1)}, u32[]{:S(2)}, u32[]{:S(2)}) %collective-permute-start.10) | collective-permute-done | bytes 80 | tf_op jit(solution)/shard_map/ppermute | solution.py:121
  (167 shorter events, 56.5 us)
Async XLA Ops:
  0.6 11.6 %copy-start.9 = (bf16[1,128,4096]{2,1,0:T(8,128)(2,1)S(1)}, bf16[1,128,4096]{2,1,0:T(8,128)(2,1)}, u32[]{:S(2)}) copy-start(bf16[1,128,4096]{2,1,0:T(8,128)(2,1)} %param.9) | copy-start | bytes 3145732
  2.0 12.8 %collective-permute-start.2 = (f32[3,4]{1,0:T(4,128)}, f32[3,4]{1,0:T(4,128)S(1)}, u32[]{:S(2)}, u32[]{:S(2)}) collective-permute-start(f32[3,4]{1,0:T(4,128)} %pad_maximum_fusion.1), channel_id=1, source_target_pairs={{0,3},{1,2},{2,1},{3,0},{4,7},{5,6},{6,5},{7,4},{8,11},{9,10},{10,... | collective-permute-start | bytes 152 | tf_op jit(solution)/shard_map/ppermute | solution.py:121
  8.6 7.7 %collective-permute-start.1 = (f32[3,4]{1,0:T(4,128)}, f32[3,4]{1,0:T(4,128)S(1)}, u32[]{:S(2)}, u32[]{:S(2)}) collective-permute-start(f32[3,4]{1,0:T(4,128)} %pad_maximum_fusion.1), channel_id=1, source_target_pairs={{0,2},{1,3},{2,0},{3,1},{4,6},{5,7},{6,4},{7,5},{8,10},{9,11},{10,... | collective-permute-start | bytes 152 | tf_op jit(solution)/shard_map/ppermute | solution.py:121
  9.2 7.1 %collective-permute-start = (f32[3,4]{1,0:T(4,128)}, f32[3,4]{1,0:T(4,128)S(1)}, u32[]{:S(2)}, u32[]{:S(2)}) collective-permute-start(f32[3,4]{1,0:T(4,128)} %pad_maximum_fusion.1), channel_id=1, source_target_pairs={{0,1},{1,0},{2,3},{3,2},{4,5},{5,4},{6,7},{7,6},{8,9},{9,8},{10,11... | collective-permute-start | bytes 152 | tf_op jit(solution)/shard_map/ppermute | solution.py:121
  14.7 9.1 %copy-start.15 = (f32[1,64,128]{2,1,0:T(8,128)S(1)}, f32[1,64,128]{2,1,0:T(8,128)}, u32[]{:S(2)}) copy-start(f32[1,64,128]{2,1,0:T(8,128)} %param.12) | copy-start | bytes 98308
  14.7 10.3 %copy-start.8 = (bf16[1,128,512]{1,2,0:T(8,128)(2,1)S(1)}, bf16[1,128,512]{1,2,0:T(8,128)(2,1)}, u32[]{:S(2)}) copy-start(bf16[1,128,512]{1,2,0:T(8,128)(2,1)} %copy-done.7) | copy-start | bytes 393220
  14.8 12.2 %copy-start = (f32[1,128,4096]{1,2,0:T(8,128)}, f32[1,128,4096]{1,2,0:T(8,128)S(1)}, u32[]{:S(2)}) copy-start(f32[1,128,4096]{1,2,0:T(8,128)S(1)} %convert_element_type.109) | copy-start | bytes 6291460
  16.5 4.2 %collective-permute-start.5 = (f32[3,16]{1,0:T(4,128)S(1)}, f32[3,16]{1,0:T(4,128)S(1)}, u32[]{:S(2)}, u32[]{:S(2)}) collective-permute-start(f32[3,16]{1,0:T(4,128)S(1)} %pad_maximum_fusion.2), channel_id=1, source_target_pairs={{0,12},{1,13},{2,14},{3,15},{4,8},{5,9},{6,10},{7,11},{8,4},{9,5},... | collective-permute-start | bytes 584 | tf_op jit(solution)/shard_map/ppermute | solution.py:121
  18.0 5.1 %collective-permute-start.4 = (f32[3,16]{1,0:T(4,128)S(1)}, f32[3,16]{1,0:T(4,128)S(1)}, u32[]{:S(2)}, u32[]{:S(2)}) collective-permute-start(f32[3,16]{1,0:T(4,128)S(1)} %pad_maximum_fusion.2), channel_id=1, source_target_pairs={{0,8},{1,9},{2,10},{3,11},{4,12},{5,13},{6,14},{7,15},{8,0},{9,1},... | collective-permute-start | bytes 584 | tf_op jit(solution)/shard_map/ppermute | solution.py:121
  19.1 4.0 %collective-permute-start.3 = (f32[3,16]{1,0:T(4,128)S(1)}, f32[3,16]{1,0:T(4,128)S(1)}, u32[]{:S(2)}, u32[]{:S(2)}) collective-permute-start(f32[3,16]{1,0:T(4,128)S(1)} %pad_maximum_fusion.2), channel_id=1, source_target_pairs={{0,4},{1,5},{2,6},{3,7},{4,0},{5,1},{6,2},{7,3},{8,12},{9,13},{10,... | collective-permute-start | bytes 584 | tf_op jit(solution)/shard_map/ppermute | solution.py:121
  37.1 6.3 %copy-start.22 = (f32[64]{0:T(128)S(1)}, f32[64]{0:T(128)}, u32[]{:S(2)}) copy-start(f32[64]{0:T(128)} %copy-done.21) | copy-start | bytes 772
  37.1 6.7 %copy-start.6 = (f32[128,8,64]{0,2,1:T(8,128)S(1)}, f32[128,8,64]{0,2,1:T(8,128)}, u32[]{:S(2)}) copy-start(f32[128,8,64]{0,2,1:T(8,128)} %convert_element_type.98) | copy-start | bytes 786436
  37.1 49.3 %all-to-all-start = ((f32[16,264,128]{2,1,0:T(8,128)}), f32[16,264,128]{2,1,0:T(8,128)}, u32[]{:S(2)}, u32[]{:S(2)}) async-start(f32[16,264,128]{2,1,0:T(8,128)} %maximum_maximum_fusion), calls=%async_computation | async-start | bytes 4325376 | tf_op jit(solution)/shard_map/all_to_all | solution.py:93
  99.0 11.0 %copy-start.34 = (f32[64]{0:T(128)S(1)}, f32[64]{0:T(128)}, u32[]{:S(2)}) copy-start(f32[64]{0:T(128)} %copy-done.33) | copy-start | bytes 772
  99.0 53.0 %all-to-all-start.1 = ((f32[16,256,128]{2,1,0:T(8,128)}), f32[16,256,128]{2,1,0:T(8,128)}, u32[]{:S(2)}, u32[]{:S(2)}) async-start(f32[16,256,128]{2,1,0:T(8,128)} %pad_maximum_fusion), calls=%async_computation.1 | async-start | bytes 4194304 | tf_op jit(solution)/shard_map/all_to_all | solution.py:112
  178.7 13.0 %copy-start.11 = (f32[128,8,64]{0,2,1:T(8,128)S(1)}, f32[128,8,64]{0,2,1:T(8,128)}, u32[]{:S(2)}) copy-start(f32[128,8,64]{0,2,1:T(8,128)} %convolution_bitcast_fusion.1) | copy-start | bytes 786436
  178.7 13.1 %copy-start.10 = (f32[128,8,64]{0,2,1:T(8,128)S(1)}, f32[128,8,64]{0,2,1:T(8,128)}, u32[]{:S(2)}) copy-start(f32[128,8,64]{0,2,1:T(8,128)} %convolution_bitcast_fusion) | copy-start | bytes 786436
  182.7 17.7 %all-to-all-start.2 = ((f32[16,3,4]{2,1,0:T(4,128)}), f32[16,3,4]{2,1,0:T(4,128)S(1)}, u32[]{:S(2)}, u32[]{:S(2)}) async-start(f32[16,3,4]{2,1,0:T(4,128)} %copy.131), calls=%async_computation.2 | async-start | bytes 65536 | tf_op jit(solution)/shard_map/all_to_all | solution.py:183
  200.4 5.3 %collective-permute-start.8 = (f32[3,4]{1,0:T(4,128)S(1)}, f32[3,4]{1,0:T(4,128)S(1)}, u32[]{:S(2)}, u32[]{:S(2)}) collective-permute-start(f32[3,4]{1,0:T(4,128)S(1)} %reduce_sum.176), channel_id=1, source_target_pairs={{0,48},{16,32},{32,16},{48,0},{64,112},{80,96},{96,80},{112,64},{1... | collective-permute-start | bytes 152 | tf_op jit(solution)/shard_map/ppermute | solution.py:121
  204.1 5.1 %collective-permute-start.7 = (f32[3,4]{1,0:T(4,128)S(1)}, f32[3,4]{1,0:T(4,128)S(1)}, u32[]{:S(2)}, u32[]{:S(2)}) collective-permute-start(f32[3,4]{1,0:T(4,128)S(1)} %reduce_sum.176), channel_id=1, source_target_pairs={{0,32},{16,48},{32,0},{48,16},{64,96},{80,112},{96,64},{112,80},{1... | collective-permute-start | bytes 152 | tf_op jit(solution)/shard_map/ppermute | solution.py:121
  204.8 4.4 %collective-permute-start.6 = (f32[3,4]{1,0:T(4,128)S(1)}, f32[3,4]{1,0:T(4,128)S(1)}, u32[]{:S(2)}, u32[]{:S(2)}) collective-permute-start(f32[3,4]{1,0:T(4,128)S(1)} %reduce_sum.176), channel_id=1, source_target_pairs={{0,16},{16,0},{32,48},{48,32},{64,80},{80,64},{96,112},{112,96},{1... | collective-permute-start | bytes 152 | tf_op jit(solution)/shard_map/ppermute | solution.py:121
  209.2 7.3 %collective-permute-start.11 = (f32[3,4]{1,0:T(4,128)S(1)}, f32[3,4]{1,0:T(4,128)S(1)}, u32[]{:S(2)}, u32[]{:S(2)}) collective-permute-start(f32[3,4]{1,0:T(4,128)S(1)} %add_add_fusion.1), channel_id=1, source_target_pairs={{0,192},{16,208},{32,224},{48,240},{64,128},{80,144},{96,160},{112... | collective-permute-start | bytes 152 | tf_op jit(solution)/shard_map/ppermute | solution.py:121
  215.0 4.5 %collective-permute-start.10 = (f32[3,4]{1,0:T(4,128)S(1)}, f32[3,4]{1,0:T(4,128)S(1)}, u32[]{:S(2)}, u32[]{:S(2)}) collective-permute-start(f32[3,4]{1,0:T(4,128)S(1)} %add_add_fusion.1), channel_id=1, source_target_pairs={{0,128},{16,144},{32,160},{48,176},{64,192},{80,208},{96,224},{112... | collective-permute-start | bytes 152 | tf_op jit(solution)/shard_map/ppermute | solution.py:121
  216.0 3.6 %collective-permute-start.9 = (f32[3,4]{1,0:T(4,128)S(1)}, f32[3,4]{1,0:T(4,128)S(1)}, u32[]{:S(2)}, u32[]{:S(2)}) collective-permute-start(f32[3,4]{1,0:T(4,128)S(1)} %add_add_fusion.1), channel_id=1, source_target_pairs={{0,64},{16,80},{32,96},{48,112},{64,0},{80,16},{96,32},{112,48},{1... | collective-permute-start | bytes 152 | tf_op jit(solution)/shard_map/ppermute | solution.py:121
  (27 other events, 79.3 us)

commit v3 on v2

--- a/solution.py
+++ b/solution.py
@@ -104,8 +104,8 @@
     same = jnp.eye(share, dtype=chain.dtype)
     spread = (chain[:, :, :, None] * same[None, None]).transpose(0, 2, 1, 3)
     spread = spread.reshape(count * share, count * share)
-    entering = jnp.einsum("ab,brl->arl", spread, states, precision=highest)
-    leaving = jnp.einsum("ba,brl->arl", spread, sources, precision=highest)
+    entering = jnp.einsum("ab,brl->arl", spread, states, precision=fast)
+    leaving = jnp.einsum("ba,brl->arl", spread, sources, precision=fast)
     back = jnp.concatenate(
         [entering.reshape(count, block, 128), leaving.reshape(count, block, 128)], axis=1
     )

time: 221 us -> 220 us (level)
  no operation moved by 1% of the time
where the time goes in v3:
time: 220 us; the launch traced here: 219 us
  waiting for transfers between devices  76.5 us (35%)
  starting transfers between devices  49 us (22%)
  matrix products  40.4 us (18%)
  local copies, waits for them, and re-layouts  30.9 us (14%)
  other arithmetic  21 us (10%)
    all_to_all x1, waiting for transfers between devices, carry_across(): lax.all_to_all(back.reshape(count * 2 * block, 128), 'ctx', 0, 0, tiled=T...  41 us
    all_to_all x1, waiting for transfers between devices, carry_across(): lax.all_to_all(payload.reshape(count * chunk, 128), 'ctx', 0, 0, tiled=True)  23.8 us
    ppermute x12, starting transfers between devices, exchange(): return lax.ppermute(value, axis, [(i, i ^ distance) for i in range(count)])  22.9 us
    ppermute x12, waiting for transfers between devices, exchange(): return lax.ppermute(value, axis, [(i, i ^ distance) for i in range(count)])  11.6 us
    dot_general x2, matrix products, slab_local(): local_part = jnp.einsum('gjqk,kgjp->qgjp', mixed, scaled, precision=fast)  11.2 us
    all_to_all x1, starting transfers between devices, carry_across(): lax.all_to_all(back.reshape(count * 2 * block, 128), 'ctx', 0, 0, tiled=T...  10.9 us
    all_to_all x1, starting transfers between devices, per_device(): own_totals = jnp.sum(lax.all_to_all(dealt, 'dp', 0, 0, tiled=True), axis=0)  8.97 us
    unnamed x79, local copies, waits for them, and re-layouts  8.16 us
  transfers between devices with their start and end apart: 15, of which 9 were waited for; matrix products, arithmetic and copies ran while one was open for 15% of the time, Pallas kernels for 0%

profile of v3, /device:TPU:2, one launch (start us, length us, event | category | flops | bytes accessed | tf_op | source)
XLA Modules:
  0.0 219.2 jit_solution(15903928091319578966)
XLA Ops:
  2.0 6.6 %collective-permute-start.2 = (f32[3,4]{1,0:T(4,128)}, f32[3,4]{1,0:T(4,128)S(1)}, u32[]{:S(2)}, u32[]{:S(2)}) collective-permute-start(f32[3,4]{1,0:T(4,128)} %pad_maximum_fusion.1), channel_id=1, source_target_pairs={{0,3},{1,2},{2,1},{3,0},{4,7},{5,6},{6,5},{7,4},{8,11},{9,10},{10,... | collective-permute-start | bytes 152 | tf_op jit(solution)/shard_map/ppermute | solution.py:121
  31.6 2.6 %reshape.315 = f32[16,128,128]{2,1,0:T(8,128)} reshape(f32[64,64,64]{2,1,0:T(8,128)} %bitcast.230) | data formatting | bytes 2097152 | tf_op jit(solution)/shard_map/reshape | solution.py:86
  34.3 2.8 %maximum_maximum_fusion = f32[16,264,128]{2,1,0:T(8,128)} fusion(f32[16,4,128]{2,1,0:T(4,128)S(1)} %broadcast_in_dim.46, f32[16,128,128]{2,1,0:T(8,128)} %reshape.315, f32[16,128,128]{2,1,0:T(8,128)S(1)} %reshape.314, f32[264]{0:T(512)S(1)} %pad.16.clone), kind=kLoop, calls=%fused_computation.8 | loop fusion | flops 1622016 | bytes 4293664 | tf_op jit(solution)/shard_map/concatenate | solution.py:91
  37.1 6.2 %all-to-all-start = ((f32[16,264,128]{2,1,0:T(8,128)}), f32[16,264,128]{2,1,0:T(8,128)}, u32[]{:S(2)}, u32[]{:S(2)}) async-start(f32[16,264,128]{2,1,0:T(8,128)} %maximum_maximum_fusion), calls=%async_computation | async-start | bytes 4325376 | tf_op jit(solution)/shard_map/all_to_all | solution.py:93
  44.5 4.7 %fusion = f32[8,8,64,128]{3,2,1,0:T(8,128)S(1)} fusion(f32[8,8,64,128]{3,2,1,0:T(8,128)} %bitcast.225, f32[8,128,128]{2,1,0:T(8,128)S(1)} %fusion.99, f32[8,8,128]{2,1,0:T(8,128)S(1)} %convolution_bitcast_fusion.2, pred[128,128]{1,0:T(8,128)(4,1)S(1)} %iota_compare_fusion), kind=kOutput, calls=%fused_computation.2 | convolution fusion | flops 406847488 | bytes 4767744 | tf_op jit(solution)/shard_map/transpose(jvp(gjqk,kgjp->qgjp))/dot_general | solution.py:41
  49.1 2.5 %multiply_reduce_fusion.1 = (f32[64]{0:T(128)S(1)}, f32[128,64]{0,1:T(8,128)S(1)}, f32[128,64,64]{0,2,1:T(8,128)}, f32[128,64,64]{0,2,1:T(8,128)S(1)}) fusion(f32[128,64,64]{0,2,1:T(8,128)S(1)} %bitcast.228, f32[128,64,64]{0,2,1:T(8,128)S(1)} %bitcast.221, f32[8,8,64,128]{3,2,1,0:T(8,128)S(1)} %fusion, f32[128,64]{0,1:T(8,128)S(1)} %fusion.89, ...), kind=kLoop, calls=%fused_computation.32 | loop fusion | flops 4186048 | bytes 10551808 | tf_op jit(solution)/shard_map/transpose(jvp())/reduce_sum | solution.py:42
  51.7 6.5 %fusion.5 = (f32[8,8,128]{2,1,0:T(8,128)S(1)}, f32[8,8,128]{2,1,0:T(8,128)S(1)}, f32[8,128,128]{2,1,0:T(8,128)S(1)}) fusion(f32[8,128,128]{2,1,0:T(8,128)S(1)} %fusion.99, f32[8,8,128]{2,1,0:T(8,128)S(1)} %convolution_bitcast_fusion.2, pred[128,128]{1,0:T(8,128)(4,1)S(1)} %iota_compare_fusion, f32[8,8,64,128]{3,2,1,0:T(8,128)S(1)} %bitcast.229, ...), kind=kOutput, calls=%fused_computation.7 | convolution fusion | flops 414040064 | bytes 5357568 | tf_op jit(solution)/shard_map/transpose(jvp(gjqk,kgjp->qgjp))/dot_general | solution.py:41
  62.6 23.8 %all-to-all-done = f32[16,264,128]{2,1,0:T(8,128)} async-done(((f32[16,264,128]{2,1,0:T(8,128)}), f32[16,264,128]{2,1,0:T(8,128)}, u32[]{:S(2)}, u32[]{:S(2)}) %all-to-all-start) | async-done | bytes 2162720 | tf_op jit(solution)/shard_map/all_to_all | solution.py:93
  87.2 3.1 %fusion.96 = (f32[16,128,128]{2,1,0:T(8,128)}, f32[16,128,128]{2,1,0:T(8,128)}) fusion(f32[16,264,128]{2,1,0:T(8,128)} %bitcast.37), kind=kLoop, calls=%fused_computation.156 | loop fusion | bytes 4194304 | tf_op jit(solution)/shard_map/slice | solution.py:96
  91.7 2.5 %fusion.44 = f32[64,32,128]{2,0,1:T(8,128)S(1)} fusion(f32[64,64,1]{1,0,2:T(8,128)S(1)} %reshape.335, f32[64,32,128]{2,1,0:T(8,128)} %bitcast.234), kind=kOutput, calls=%fused_computation.54 | convolution fusion | flops 100663296 | bytes 2113536 | tf_op jit(solution)/shard_map/ab,brl->arl/dot_general | solution.py:107
  98.1 10.9 %all-to-all-start.1 = ((f32[16,256,128]{2,1,0:T(8,128)}), f32[16,256,128]{2,1,0:T(8,128)}, u32[]{:S(2)}, u32[]{:S(2)}) async-start(f32[16,256,128]{2,1,0:T(8,128)} %pad_maximum_fusion), calls=%async_computation.1 | async-start | bytes 4194304 | tf_op jit(solution)/shard_map/all_to_all | solution.py:112
  110.1 41.0 %all-to-all-done.1 = f32[16,256,128]{2,1,0:T(8,128)} async-done(((f32[16,256,128]{2,1,0:T(8,128)}), f32[16,256,128]{2,1,0:T(8,128)}, u32[]{:S(2)}, u32[]{:S(2)}) %all-to-all-start.1) | async-done | bytes 2097184 | tf_op jit(solution)/shard_map/all_to_all | solution.py:112
  151.2 3.2 %slice_multiply_fusion = (f32[16,128,128]{2,1,0:T(8,128)}, f32[16,128,128]{2,1,0:T(8,128)}, f32[16,128,128]{2,1,0:T(8,128)S(1)}) fusion(f32[16,256,128]{2,1,0:T(8,128)} %all-to-all-done.1), kind=kLoop, calls=%fused_computation.151 | loop fusion | flops 262144 | bytes 5242880 | tf_op jit(solution)/shard_map/transpose(jvp())/mul | solution.py:53
  154.4 2.7 %mul.284 = f32[64,64,64]{2,1,0:T(8,128)} reshape(f32[16,128,128]{2,1,0:T(8,128)} %get-tuple-element.110) | data formatting | bytes 2097152 | tf_op jit(solution)/shard_map/transpose(jvp())/mul | solution.py:53
  157.1 2.7 %reduce_sum.167 = f32[64]{0:T(128)} reduce(f32[64,64,64]{2,1,0:T(8,128)} %mul.284, f32[]{:T(128)} %constant.81.clone.1), dimensions={1,2}, to_apply=%region_10.12 | reduce | flops 262080 | bytes 1048836 | tf_op jit(solution)/shard_map/transpose(jvp())/reduce_sum | solution.py:53
  164.5 2.7 %reshape_reshape.8 = f32[8,8,64,64]{3,2,1,0:T(8,128)} reshape(f32[16,128,128]{2,1,0:T(8,128)} %get-tuple-element.111) | data formatting | bytes 2097152 | tf_op jit(solution)/shard_map/jvp()/reshape;reshape | solution.py:54
  167.2 3.6 %fusion.8 = f32[128,8,8]{0,2,1:T(8,128)} fusion(f32[128,8,8,64]{0,3,2,1:T(8,128)} %bitcast.226, f32[8,8,64,64]{3,2,1,0:T(8,128)} %reshape_reshape.8, bf16[128,8,64,1]{0,2,3,1:T(8,128)(2,1)S(1)} %bitcast.239), kind=kOutput, calls=%fused_computation.14 | convolution fusion | flops 202366976 | bytes 3309568 | tf_op jit(solution)/shard_map/jvp(qgn,gjpn->qgjp)/dot_general | solution.py:55
  173.4 4.3 %fusion.13 = (f32[128,8,8]{0,2,1:T(8,128)S(1)}, f32[8,8,64,128]{3,2,1,0:T(8,128)}) fusion(f32[128,8,8,64]{0,3,2,1:T(8,128)S(1)} %bitcast.222, f32[8,8,64,64]{3,2,1,0:T(8,128)} %reshape_reshape.7, f32[128,8,8]{0,2,1:T(8,128)S(1)} %bitcast.245, f32[128,8,64]{0,2,1:T(8,128)S(1)} %convert_element_type.97), kind=kOutput, calls=%fused_computation.22 | convolution fusion | flops 202891264 | bytes 5570560 | tf_op jit(solution)/shard_map/transpose(jvp(kgjn,kgjp->gjpn))/dot_general | solution.py:51
  181.8 9.0 %all-to-all-start.2 = ((f32[16,3,4]{2,1,0:T(4,128)}), f32[16,3,4]{2,1,0:T(4,128)S(1)}, u32[]{:S(2)}, u32[]{:S(2)}) async-start(f32[16,3,4]{2,1,0:T(4,128)} %copy.131), calls=%async_computation.2 | async-start | bytes 65536 | tf_op jit(solution)/shard_map/all_to_all | solution.py:183
  190.9 4.3 %fusion.36 = bf16[128,8,64]{0,2,1:T(8,128)(2,1)S(1)} fusion(f32[128,8,64]{0,2,1:T(8,128)S(1)} %copy-done.10, f32[8,8,64,64]{3,2,1,0:T(8,128)} %reshape_reshape.8, f32[128,8,8,64]{0,3,2,1:T(8,128)} %bitcast.227, f32[128,8,8]{0,2,1:T(8,128)S(1)} %bitcast.247), kind=kOutput, calls=%fused_computation.46 | convolution fusion | flops 201981952 | bytes 3571712 | tf_op jit(solution)/shard_map/transpose(jvp(qgn,gjpn->qgjp))/dot_general | solution.py:55
  199.5 3.8 %collective-permute-start.8 = (f32[3,4]{1,0:T(4,128)S(1)}, f32[3,4]{1,0:T(4,128)S(1)}, u32[]{:S(2)}, u32[]{:S(2)}) collective-permute-start(f32[3,4]{1,0:T(4,128)S(1)} %reduce_sum.176), channel_id=1, source_target_pairs={{0,48},{16,32},{32,16},{48,0},{64,112},{80,96},{96,80},{112,64},{1... | collective-permute-start | bytes 152 | tf_op jit(solution)/shard_map/ppermute | solution.py:121
  204.8 3.5 %collective-permute-done.7 = f32[3,4]{1,0:T(4,128)S(1)} collective-permute-done((f32[3,4]{1,0:T(4,128)S(1)}, f32[3,4]{1,0:T(4,128)S(1)}, u32[]{:S(2)}, u32[]{:S(2)}) %collective-permute-start.7) | collective-permute-done | bytes 80 | tf_op jit(solution)/shard_map/ppermute | solution.py:121
  208.4 5.8 %collective-permute-start.11 = (f32[3,4]{1,0:T(4,128)S(1)}, f32[3,4]{1,0:T(4,128)S(1)}, u32[]{:S(2)}, u32[]{:S(2)}) collective-permute-start(f32[3,4]{1,0:T(4,128)S(1)} %add_add_fusion.1), channel_id=1, source_target_pairs={{0,192},{16,208},{32,224},{48,240},{64,128},{80,144},{96,160},{112... | collective-permute-start | bytes 152 | tf_op jit(solution)/shard_map/ppermute | solution.py:121
  215.7 2.9 %collective-permute-done.10 = f32[3,4]{1,0:T(4,128)S(1)} collective-permute-done((f32[3,4]{1,0:T(4,128)S(1)}, f32[3,4]{1,0:T(4,128)S(1)}, u32[]{:S(2)}, u32[]{:S(2)}) %collective-permute-start.10) | collective-permute-done | bytes 80 | tf_op jit(solution)/shard_map/ppermute | solution.py:121
  (167 shorter events, 56.0 us)
Async XLA Ops:
  0.6 11.6 %copy-start.9 = (bf16[1,128,4096]{2,1,0:T(8,128)(2,1)S(1)}, bf16[1,128,4096]{2,1,0:T(8,128)(2,1)}, u32[]{:S(2)}) copy-start(bf16[1,128,4096]{2,1,0:T(8,128)(2,1)} %param.9) | copy-start | bytes 3145732
  2.0 12.8 %collective-permute-start.2 = (f32[3,4]{1,0:T(4,128)}, f32[3,4]{1,0:T(4,128)S(1)}, u32[]{:S(2)}, u32[]{:S(2)}) collective-permute-start(f32[3,4]{1,0:T(4,128)} %pad_maximum_fusion.1), channel_id=1, source_target_pairs={{0,3},{1,2},{2,1},{3,0},{4,7},{5,6},{6,5},{7,4},{8,11},{9,10},{10,... | collective-permute-start | bytes 152 | tf_op jit(solution)/shard_map/ppermute | solution.py:121
  8.6 7.7 %collective-permute-start.1 = (f32[3,4]{1,0:T(4,128)}, f32[3,4]{1,0:T(4,128)S(1)}, u32[]{:S(2)}, u32[]{:S(2)}) collective-permute-start(f32[3,4]{1,0:T(4,128)} %pad_maximum_fusion.1), channel_id=1, source_target_pairs={{0,2},{1,3},{2,0},{3,1},{4,6},{5,7},{6,4},{7,5},{8,10},{9,11},{10,... | collective-permute-start | bytes 152 | tf_op jit(solution)/shard_map/ppermute | solution.py:121
  9.2 7.1 %collective-permute-start = (f32[3,4]{1,0:T(4,128)}, f32[3,4]{1,0:T(4,128)S(1)}, u32[]{:S(2)}, u32[]{:S(2)}) collective-permute-start(f32[3,4]{1,0:T(4,128)} %pad_maximum_fusion.1), channel_id=1, source_target_pairs={{0,1},{1,0},{2,3},{3,2},{4,5},{5,4},{6,7},{7,6},{8,9},{9,8},{10,11... | collective-permute-start | bytes 152 | tf_op jit(solution)/shard_map/ppermute | solution.py:121
  14.7 9.1 %copy-start.15 = (f32[1,64,128]{2,1,0:T(8,128)S(1)}, f32[1,64,128]{2,1,0:T(8,128)}, u32[]{:S(2)}) copy-start(f32[1,64,128]{2,1,0:T(8,128)} %param.12) | copy-start | bytes 98308
  14.7 10.3 %copy-start.8 = (bf16[1,128,512]{1,2,0:T(8,128)(2,1)S(1)}, bf16[1,128,512]{1,2,0:T(8,128)(2,1)}, u32[]{:S(2)}) copy-start(bf16[1,128,512]{1,2,0:T(8,128)(2,1)} %copy-done.7) | copy-start | bytes 393220
  14.8 12.2 %copy-start = (f32[1,128,4096]{1,2,0:T(8,128)}, f32[1,128,4096]{1,2,0:T(8,128)S(1)}, u32[]{:S(2)}) copy-start(f32[1,128,4096]{1,2,0:T(8,128)S(1)} %convert_element_type.109) | copy-start | bytes 6291460
  16.5 4.2 %collective-permute-start.5 = (f32[3,16]{1,0:T(4,128)S(1)}, f32[3,16]{1,0:T(4,128)S(1)}, u32[]{:S(2)}, u32[]{:S(2)}) collective-permute-start(f32[3,16]{1,0:T(4,128)S(1)} %pad_maximum_fusion.2), channel_id=1, source_target_pairs={{0,12},{1,13},{2,14},{3,15},{4,8},{5,9},{6,10},{7,11},{8,4},{9,5},... | collective-permute-start | bytes 584 | tf_op jit(solution)/shard_map/ppermute | solution.py:121
  18.0 5.1 %collective-permute-start.4 = (f32[3,16]{1,0:T(4,128)S(1)}, f32[3,16]{1,0:T(4,128)S(1)}, u32[]{:S(2)}, u32[]{:S(2)}) collective-permute-start(f32[3,16]{1,0:T(4,128)S(1)} %pad_maximum_fusion.2), channel_id=1, source_target_pairs={{0,8},{1,9},{2,10},{3,11},{4,12},{5,13},{6,14},{7,15},{8,0},{9,1},... | collective-permute-start | bytes 584 | tf_op jit(solution)/shard_map/ppermute | solution.py:121
  19.1 4.0 %collective-permute-start.3 = (f32[3,16]{1,0:T(4,128)S(1)}, f32[3,16]{1,0:T(4,128)S(1)}, u32[]{:S(2)}, u32[]{:S(2)}) collective-permute-start(f32[3,16]{1,0:T(4,128)S(1)} %pad_maximum_fusion.2), channel_id=1, source_target_pairs={{0,4},{1,5},{2,6},{3,7},{4,0},{5,1},{6,2},{7,3},{8,12},{9,13},{10,... | collective-permute-start | bytes 584 | tf_op jit(solution)/shard_map/ppermute | solution.py:121
  37.1 6.3 %copy-start.22 = (f32[64]{0:T(128)S(1)}, f32[64]{0:T(128)}, u32[]{:S(2)}) copy-start(f32[64]{0:T(128)} %copy-done.21) | copy-start | bytes 772
  37.1 6.7 %copy-start.6 = (f32[128,8,64]{0,2,1:T(8,128)S(1)}, f32[128,8,64]{0,2,1:T(8,128)}, u32[]{:S(2)}) copy-start(f32[128,8,64]{0,2,1:T(8,128)} %convert_element_type.98) | copy-start | bytes 786436
  37.1 49.3 %all-to-all-start = ((f32[16,264,128]{2,1,0:T(8,128)}), f32[16,264,128]{2,1,0:T(8,128)}, u32[]{:S(2)}, u32[]{:S(2)}) async-start(f32[16,264,128]{2,1,0:T(8,128)} %maximum_maximum_fusion), calls=%async_computation | async-start | bytes 4325376 | tf_op jit(solution)/shard_map/all_to_all | solution.py:93
  98.1 11.0 %copy-start.34 = (f32[64]{0:T(128)S(1)}, f32[64]{0:T(128)}, u32[]{:S(2)}) copy-start(f32[64]{0:T(128)} %copy-done.33) | copy-start | bytes 772
  98.1 53.0 %all-to-all-start.1 = ((f32[16,256,128]{2,1,0:T(8,128)}), f32[16,256,128]{2,1,0:T(8,128)}, u32[]{:S(2)}, u32[]{:S(2)}) async-start(f32[16,256,128]{2,1,0:T(8,128)} %pad_maximum_fusion), calls=%async_computation.1 | async-start | bytes 4194304 | tf_op jit(solution)/shard_map/all_to_all | solution.py:112
  177.8 13.0 %copy-start.11 = (f32[128,8,64]{0,2,1:T(8,128)S(1)}, f32[128,8,64]{0,2,1:T(8,128)}, u32[]{:S(2)}) copy-start(f32[128,8,64]{0,2,1:T(8,128)} %convolution_bitcast_fusion.1) | copy-start | bytes 786436
  177.8 13.1 %copy-start.10 = (f32[128,8,64]{0,2,1:T(8,128)S(1)}, f32[128,8,64]{0,2,1:T(8,128)}, u32[]{:S(2)}) copy-start(f32[128,8,64]{0,2,1:T(8,128)} %convolution_bitcast_fusion) | copy-start | bytes 786436
  181.8 17.7 %all-to-all-start.2 = ((f32[16,3,4]{2,1,0:T(4,128)}), f32[16,3,4]{2,1,0:T(4,128)S(1)}, u32[]{:S(2)}, u32[]{:S(2)}) async-start(f32[16,3,4]{2,1,0:T(4,128)} %copy.131), calls=%async_computation.2 | async-start | bytes 65536 | tf_op jit(solution)/shard_map/all_to_all | solution.py:183
  199.5 5.3 %collective-permute-start.8 = (f32[3,4]{1,0:T(4,128)S(1)}, f32[3,4]{1,0:T(4,128)S(1)}, u32[]{:S(2)}, u32[]{:S(2)}) collective-permute-start(f32[3,4]{1,0:T(4,128)S(1)} %reduce_sum.176), channel_id=1, source_target_pairs={{0,48},{16,32},{32,16},{48,0},{64,112},{80,96},{96,80},{112,64},{1... | collective-permute-start | bytes 152 | tf_op jit(solution)/shard_map/ppermute | solution.py:121
  203.3 5.1 %collective-permute-start.7 = (f32[3,4]{1,0:T(4,128)S(1)}, f32[3,4]{1,0:T(4,128)S(1)}, u32[]{:S(2)}, u32[]{:S(2)}) collective-permute-start(f32[3,4]{1,0:T(4,128)S(1)} %reduce_sum.176), channel_id=1, source_target_pairs={{0,32},{16,48},{32,0},{48,16},{64,96},{80,112},{96,64},{112,80},{1... | collective-permute-start | bytes 152 | tf_op jit(solution)/shard_map/ppermute | solution.py:121
  204.0 4.4 %collective-permute-start.6 = (f32[3,4]{1,0:T(4,128)S(1)}, f32[3,4]{1,0:T(4,128)S(1)}, u32[]{:S(2)}, u32[]{:S(2)}) collective-permute-start(f32[3,4]{1,0:T(4,128)S(1)} %reduce_sum.176), channel_id=1, source_target_pairs={{0,16},{16,0},{32,48},{48,32},{64,80},{80,64},{96,112},{112,96},{1... | collective-permute-start | bytes 152 | tf_op jit(solution)/shard_map/ppermute | solution.py:121
  208.4 7.3 %collective-permute-start.11 = (f32[3,4]{1,0:T(4,128)S(1)}, f32[3,4]{1,0:T(4,128)S(1)}, u32[]{:S(2)}, u32[]{:S(2)}) collective-permute-start(f32[3,4]{1,0:T(4,128)S(1)} %add_add_fusion.1), channel_id=1, source_target_pairs={{0,192},{16,208},{32,224},{48,240},{64,128},{80,144},{96,160},{112... | collective-permute-start | bytes 152 | tf_op jit(solution)/shard_map/ppermute | solution.py:121
  214.1 4.5 %collective-permute-start.10 = (f32[3,4]{1,0:T(4,128)S(1)}, f32[3,4]{1,0:T(4,128)S(1)}, u32[]{:S(2)}, u32[]{:S(2)}) collective-permute-start(f32[3,4]{1,0:T(4,128)S(1)} %add_add_fusion.1), channel_id=1, source_target_pairs={{0,128},{16,144},{32,160},{48,176},{64,192},{80,208},{96,224},{112... | collective-permute-start | bytes 152 | tf_op jit(solution)/shard_map/ppermute | solution.py:121
  215.1 3.6 %collective-permute-start.9 = (f32[3,4]{1,0:T(4,128)S(1)}, f32[3,4]{1,0:T(4,128)S(1)}, u32[]{:S(2)}, u32[]{:S(2)}) collective-permute-start(f32[3,4]{1,0:T(4,128)S(1)} %add_add_fusion.1), channel_id=1, source_target_pairs={{0,64},{16,80},{32,96},{48,112},{64,0},{80,16},{96,32},{112,48},{1... | collective-permute-start | bytes 152 | tf_op jit(solution)/shard_map/ppermute | solution.py:121
  (27 other events, 78.8 us)

commit v4 on v3

--- a/solution.py
+++ b/solution.py
@@ -162,11 +162,8 @@
     c = c_proj[0].astype(jnp.float32).reshape(tokens, G, N)
     raw = dt_raw[0]
     total, local_state, local_source = slab_terms(x, b, c, raw, bias_all, alog_all, grad)
-    (total, local_state, local_source), late = lax.optimization_barrier(
-        ((total, local_state, local_source), (x, b, c, raw, bias_all, alog_all, skip_all, grad))
-    )
-    _, local_pullback = jax.vjp(slab_local, *late[:7])
-    local_grads = local_pullback(late[7])
+    _, local_pullback = jax.vjp(slab_local, x, b, c, raw, bias_all, alog_all, skip_all)
+    local_grads = local_pullback(grad)
     entering, leaving, local_grads = carry_across(total, local_state, local_source, local_grads)
     _, carry_pullback = jax.vjp(slab_carry, x, b, c, raw, bias_all, alog_all, entering)
     carry_grads = carry_pullback((grad, leaving))[:6]

time: 220 us -> 244 us (1.11)
  waiting for transfers between devices: 76.5 us -> 85.8 us
  other arithmetic: 21 us -> 28.4 us
  local copies, waits for them, and re-layouts: 30.9 us -> 36.1 us
    all_to_all x1, waiting for transfers between devices: 23.8 us -> 33.1 us  [carry_across(): lax.all_to_all(payload.reshape(count * chunk, 128), 'ctx', 0, 0, tiled=True)]
    another operation x0 -> x2, local copies, waits for them, and re-layouts: none -> 5.18 us  [the longest x1 2.6 us: carry_across(): sources = local_source.reshape(count, block, 128)]
    reshape x2 -> x0, local copies, waits for them, and re-layouts: 4.38 us -> none  [the longest x1 2.58 us: carry_across(): sources = local_source.reshape(count, block, 128)]
    dot_general x2, matrix products: 7.94 us -> 4.32 us  [slab_carry(): cross_part = jnp.einsum('qgn,gjpn->qgjp', c, entering, precision=fast)]
    add_any x0 -> x1, other arithmetic: none -> 3.28 us  [slab_prelude(): x * dt_value.T[:, :, None]]
    unnamed x79 -> x65, local copies, waits for them, and re-layouts: 8.16 us -> 8.32 us
  transfers between devices with their start and end apart: 15 -> 15, of which waited for: 9 -> 9; matrix products, arithmetic and copies ran while one was open for 15% -> 11% of each run, Pallas kernels for 0% -> 0%
where the time goes in v4:
time: 244 us; the launch traced here: 242 us
  waiting for transfers between devices  85.8 us (35%)
  starting transfers between devices  49.5 us (20%)
  matrix products  41.1 us (17%)
  local copies, waits for them, and re-layouts  36.1 us (15%)
  other arithmetic  28.4 us (12%)
    all_to_all x1, waiting for transfers between devices, carry_across(): lax.all_to_all(back.reshape(count * 2 * block, 128), 'ctx', 0, 0, tiled=T...  40.6 us
    all_to_all x1, waiting for transfers between devices, carry_across(): lax.all_to_all(payload.reshape(count * chunk, 128), 'ctx', 0, 0, tiled=True)  33.1 us
    ppermute x12, starting transfers between devices, exchange(): return lax.ppermute(value, axis, [(i, i ^ distance) for i in range(count)])  23.7 us
    dot_general x2, matrix products, slab_local(): local_part = jnp.einsum('gjqk,kgjp->qgjp', mixed, scaled, precision=fast)  12.1 us
    ppermute x12, waiting for transfers between devices, exchange(): return lax.ppermute(value, axis, [(i, i ^ distance) for i in range(count)])  12.1 us
    all_to_all x1, starting transfers between devices, carry_across(): lax.all_to_all(back.reshape(count * 2 * block, 128), 'ctx', 0, 0, tiled=T...  10.7 us
    all_to_all x1, starting transfers between devices, per_device(): own_totals = jnp.sum(lax.all_to_all(dealt, 'dp', 0, 0, tiled=True), axis=0)  8.62 us
    unnamed x65, local copies, waits for them, and re-layouts  8.32 us
  transfers between devices with their start and end apart: 15, of which 9 were waited for; matrix products, arithmetic and copies ran while one was open for 11% of the time, Pallas kernels for 0%

profile of v4, /device:TPU:2, one launch (start us, length us, event | category | flops | bytes accessed | tf_op | source)
XLA Modules:
  0.0 242.1 jit_solution(1680295605169633489)
XLA Ops:
  1.5 7.3 %collective-permute-start.1 = (f32[3,4]{1,0:T(4,128)S(1)}, f32[3,4]{1,0:T(4,128)S(1)}, u32[]{:S(2)}, u32[]{:S(2)}) collective-permute-start(f32[3,4]{1,0:T(4,128)S(1)} %pad_maximum_fusion.1), channel_id=1, source_target_pairs={{0,2},{1,3},{2,0},{3,1},{4,6},{5,7},{6,4},{7,5},{8,10},{9,11},{10,... | collective-permute-start | bytes 152 | tf_op jit(solution)/shard_map/ppermute | solution.py:121
  23.8 6.0 %fusion.21 = (f32[128,8,8]{0,2,1:T(8,128)S(1)}, f32[128,8,8,64]{0,3,2,1:T(8,128)S(1)}, f32[8,8,128,64]{2,3,1,0:T(8,128)}) fusion(bf16[128,8,8,64]{0,3,2,1:T(8,128)(2,1)} %bitcast.248, bf16[8,8,64,128]{3,2,1,0:T(8,128)(2,1)S(1)} %bitcast.241, f32[8,128,128]{1,2,0:T(8,128)} %fusion.98, f32[8,8,128]{2,1,0:T(8,128)S(1)} %bitcast.265, ...), kind=kOutput, calls=%fused_computation.33 | convolution fusion | flops 408412160 | bytes 6897664 | tf_op jit(solution)/shard_map/transpose(jvp(gjqk,kgjp->qgjp))/dot_general | solution.py:41
  29.8 6.1 %fusion.9 = (f32[8,8,128]{2,1,0:T(8,128)S(1)}, f32[8,8,128]{2,1,0:T(8,128)S(1)}, f32[8,128,128]{1,2,0:T(8,128)}) fusion(f32[8,128,128]{1,2,0:T(8,128)S(1)} %copy-done.7, f32[8,8,128]{2,1,0:T(8,128)S(1)} %bitcast.266, pred[128,128]{0,1:T(8,128)(4,1)S(1)} %iota_compare_fusion, bf16[8,8,64,128]{3,2,1,0:T(8,128)(2,1)S(1)} %bitcast.242, ...), kind=kOutput, calls=%fused_computation.14 | convolution fusion | flops 414564352 | bytes 4341760 | tf_op jit(solution)/shard_map/transpose(jvp(gjqk,kgjp->qgjp))/dot_general | solution.py:41
  39.5 2.6 %reshape_reshape.14 = f32[16,128,128]{2,1,0:T(8,128)} reshape(f32[8,8,64,64]{3,2,1,0:T(8,128)} %fusion.28) | data formatting | bytes 2097152 | tf_op jit(solution)/shard_map/reshape;reshape | solution.py:85
  44.2 2.6 %reshape_reshape.15 = f32[16,128,128]{2,1,0:T(8,128)} reshape(f32[8,8,64,64]{3,2,1,0:T(8,128)} %fusion.10) | data formatting | bytes 2097152 | tf_op jit(solution)/shard_map/reshape;reshape | solution.py:86
  46.8 3.1 %maximum_maximum_fusion = f32[16,264,128]{2,1,0:T(8,128)} fusion(f32[16,4,128]{2,1,0:T(4,128)S(1)} %broadcast_in_dim.46, f32[16,128,128]{2,1,0:T(8,128)} %reshape_reshape.15, f32[16,128,128]{2,1,0:T(8,128)} %reshape_reshape.14, f32[264]{0:T(512)S(1)} %pad.16.clone), kind=kLoop, calls=%fused_computation.15 | loop fusion | flops 1622016 | bytes 4293664 | tf_op jit(solution)/shard_map/concatenate | solution.py:91
  49.9 6.5 %all-to-all-start = ((f32[16,264,128]{2,1,0:T(8,128)}), f32[16,264,128]{2,1,0:T(8,128)}, u32[]{:S(2)}, u32[]{:S(2)}) async-start(f32[16,264,128]{2,1,0:T(8,128)} %maximum_maximum_fusion), calls=%async_computation | async-start | bytes 4325376 | tf_op jit(solution)/shard_map/all_to_all | solution.py:93
  63.3 3.3 %fusion.17 = f32[128,64,64]{0,2,1:T(8,128)} fusion(f32[8,8,128,64]{2,3,1,0:T(8,128)} %get-tuple-element.107, f32[128,64]{0,1:T(8,128)S(1)} %get-tuple-element.92, f32[64]{0:T(128)S(1)} %copy-done.25, bf16[128,64,64]{0,2,1:T(8,128)(2,1)S(1)} %bitcast.244), kind=kLoop, calls=%fused_computation.25 | loop fusion | flops 2097152 | bytes 5275904 | tf_op jit(solution)/shard_map/transpose(jvp())/add_any | solution.py:27
  66.6 33.1 %all-to-all-done = f32[16,264,128]{2,1,0:T(8,128)} async-done(((f32[16,264,128]{2,1,0:T(8,128)}), f32[16,264,128]{2,1,0:T(8,128)}, u32[]{:S(2)}, u32[]{:S(2)}) %all-to-all-start) | async-done | bytes 2162720 | tf_op jit(solution)/shard_map/all_to_all | solution.py:93
  99.7 3.1 %fusion.95 = (f32[16,128,128]{2,1,0:T(8,128)}, f32[16,128,128]{2,1,0:T(8,128)}) fusion(f32[16,264,128]{2,1,0:T(8,128)} %bitcast.34), kind=kLoop, calls=%fused_computation.151 | loop fusion | bytes 4194304 | tf_op jit(solution)/shard_map/slice | solution.py:96
  114.2 10.7 %all-to-all-start.1 = ((f32[16,256,128]{2,1,0:T(8,128)}), f32[16,256,128]{2,1,0:T(8,128)}, u32[]{:S(2)}, u32[]{:S(2)}) async-start(f32[16,256,128]{2,1,0:T(8,128)} %pad_maximum_fusion), calls=%async_computation.1 | async-start | bytes 4194304 | tf_op jit(solution)/shard_map/all_to_all | solution.py:112
  126.5 40.6 %all-to-all-done.1 = f32[16,256,128]{2,1,0:T(8,128)} async-done(((f32[16,256,128]{2,1,0:T(8,128)}), f32[16,256,128]{2,1,0:T(8,128)}, u32[]{:S(2)}, u32[]{:S(2)}) %all-to-all-start.1) | async-done | bytes 2097184 | tf_op jit(solution)/shard_map/all_to_all | solution.py:112
  167.1 3.4 %slice_multiply_fusion = (f32[16,128,128]{2,1,0:T(8,128)}, f32[16,128,128]{2,1,0:T(8,128)}, f32[16,128,128]{2,1,0:T(8,128)}) fusion(f32[16,256,128]{2,1,0:T(8,128)} %all-to-all-done.1), kind=kLoop, calls=%fused_computation.146 | loop fusion | flops 262144 | bytes 5242880 | tf_op jit(solution)/shard_map/transpose(jvp())/mul | solution.py:53
  170.5 2.7 %mul.277 = f32[64,64,64]{2,1,0:T(8,128)} reshape(f32[16,128,128]{2,1,0:T(8,128)} %get-tuple-element.82) | data formatting | bytes 2097152 | tf_op jit(solution)/shard_map/transpose(jvp())/mul | solution.py:53
  173.2 2.7 %reduce_sum.188 = f32[64]{0:T(128)} reduce(f32[64,64,64]{2,1,0:T(8,128)} %mul.277, f32[]{:T(128)} %constant.81.clone.1), dimensions={1,2}, to_apply=%region_11.13 | reduce | flops 262080 | bytes 1048836 | tf_op jit(solution)/shard_map/transpose(jvp())/reduce_sum | solution.py:53
  180.1 2.7 %reshape_reshape.16 = f32[8,8,64,64]{3,2,1,0:T(8,128)} reshape(f32[16,128,128]{2,1,0:T(8,128)} %get-tuple-element.84) | data formatting | bytes 2097152 | tf_op jit(solution)/shard_map/transpose(jvp())/reshape;reshape | solution.py:52
  182.8 4.3 %fusion.19 = (f32[128,8,8]{0,2,1:T(8,128)}, f32[128,8,64]{0,2,1:T(8,128)}) fusion(f32[128,8,64]{0,2,1:T(8,128)S(1)} %copy-done.4, f32[128,8,8]{0,2,1:T(8,128)} %bitcast.263, f32[8,8,64,64]{3,2,1,0:T(8,128)} %reshape_reshape.16, f32[128,8,8,64]{0,3,2,1:T(8,128)S(1)} %get-tuple-element.79, f32[128,8,8]{0,2,1:T(8,128)} %copy-done.12), kind=kOutput, calls=%fused_computation.29 | convolution fusion | flops 203874304 | bytes 3768320 | tf_op jit(solution)/shard_map/transpose(jvp(kgjn,kgjp->gjpn))/dot_general | solution.py:51
  187.2 3.2 %fusion.20 = (f32[128,8,8]{0,2,1:T(8,128)}, f32[8,8,64,128]{3,2,1,0:T(8,128)}) fusion(f32[128,8,8,64]{0,3,2,1:T(8,128)S(1)} %get-tuple-element.79, f32[8,8,64,64]{3,2,1,0:T(8,128)S(1)} %copy-done, f32[128,8,8]{0,2,1:T(8,128)S(1)} %bitcast.264, f32[128,8,64]{0,2,1:T(8,128)S(1)} %copy-done.4), kind=kOutput, calls=%fused_computation.31 | convolution fusion | flops 202891264 | bytes 5570560 | tf_op jit(solution)/shard_map/transpose(jvp(kgjn,kgjp->gjpn))/dot_general | solution.py:51
  201.2 8.6 %all-to-all-start.2 = ((f32[16,3,4]{2,1,0:T(4,128)}), f32[16,3,4]{2,1,0:T(4,128)}, u32[]{:S(2)}, u32[]{:S(2)}) async-start(f32[16,3,4]{2,1,0:T(4,128)} %copy.156), calls=%async_computation.2 | async-start | bytes 65536 | tf_op jit(solution)/shard_map/all_to_all | solution.py:180
  211.4 2.8 %fusion.41 = bf16[128,8,64]{0,2,1:T(8,128)(2,1)S(1)} fusion(f32[128,8,64]{0,2,1:T(8,128)S(1)} %copy-done.5, f32[8,8,64,64]{3,2,1,0:T(8,128)S(1)} %reshape_reshape.17, bf16[128,8,8,64]{0,3,2,1:T(8,128)(2,1)S(1)} %bitcast.246, f32[128,8,8]{0,2,1:T(8,128)} %bitcast.268), kind=kOutput, calls=%fused_computation.52 | convolution fusion | flops 202506240 | bytes 2523136 | tf_op jit(solution)/shard_map/transpose(jvp(qgn,gjpn->qgjp))/dot_general | solution.py:55
  220.7 4.9 %collective-permute-start.7 = (f32[3,4]{1,0:T(4,128)S(1)}, f32[3,4]{1,0:T(4,128)S(1)}, u32[]{:S(2)}, u32[]{:S(2)}) collective-permute-start(f32[3,4]{1,0:T(4,128)S(1)} %reduce_sum.197), channel_id=1, source_target_pairs={{0,32},{16,48},{32,0},{48,16},{64,96},{80,112},{96,64},{112,80},{1... | collective-permute-start | bytes 152 | tf_op jit(solution)/shard_map/ppermute | solution.py:121
  227.1 3.2 %collective-permute-done.8 = f32[3,4]{1,0:T(4,128)S(1)} collective-permute-done((f32[3,4]{1,0:T(4,128)S(1)}, f32[3,4]{1,0:T(4,128)S(1)}, u32[]{:S(2)}, u32[]{:S(2)}) %collective-permute-start.8) | collective-permute-done | bytes 80 | tf_op jit(solution)/shard_map/ppermute | solution.py:121
  230.3 4.6 %collective-permute-start.10 = (f32[3,4]{1,0:T(4,128)S(1)}, f32[3,4]{1,0:T(4,128)S(1)}, u32[]{:S(2)}, u32[]{:S(2)}) collective-permute-start(f32[3,4]{1,0:T(4,128)S(1)} %add_add_fusion.1), channel_id=1, source_target_pairs={{0,128},{16,144},{32,160},{48,176},{64,192},{80,208},{96,224},{112... | collective-permute-start | bytes 152 | tf_op jit(solution)/shard_map/ppermute | solution.py:121
  234.9 3.0 %collective-permute-start.11 = (f32[3,4]{1,0:T(4,128)S(1)}, f32[3,4]{1,0:T(4,128)S(1)}, u32[]{:S(2)}, u32[]{:S(2)}) collective-permute-start(f32[3,4]{1,0:T(4,128)S(1)} %add_add_fusion.1), channel_id=1, source_target_pairs={{0,192},{16,208},{32,224},{48,240},{64,128},{80,144},{96,160},{112... | collective-permute-start | bytes 152 | tf_op jit(solution)/shard_map/ppermute | solution.py:121
  (150 shorter events, 70.0 us)
Async XLA Ops:
  0.6 11.9 %copy-start.6 = (bf16[1,128,4096]{2,1,0:T(8,128)(2,1)S(1)}, bf16[1,128,4096]{2,1,0:T(8,128)(2,1)}, u32[]{:S(2)}) copy-start(bf16[1,128,4096]{2,1,0:T(8,128)(2,1)} %param.9) | copy-start | bytes 3145732
  1.4 13.5 %collective-permute-start = (f32[3,4]{1,0:T(4,128)S(1)}, f32[3,4]{1,0:T(4,128)S(1)}, u32[]{:S(2)}, u32[]{:S(2)}) collective-permute-start(f32[3,4]{1,0:T(4,128)S(1)} %pad_maximum_fusion.1), channel_id=1, source_target_pairs={{0,1},{1,0},{2,3},{3,2},{4,5},{5,4},{6,7},{7,6},{8,9},{9,8},{10,11... | collective-permute-start | bytes 152 | tf_op jit(solution)/shard_map/ppermute | solution.py:121
  1.5 13.5 %collective-permute-start.1 = (f32[3,4]{1,0:T(4,128)S(1)}, f32[3,4]{1,0:T(4,128)S(1)}, u32[]{:S(2)}, u32[]{:S(2)}) collective-permute-start(f32[3,4]{1,0:T(4,128)S(1)} %pad_maximum_fusion.1), channel_id=1, source_target_pairs={{0,2},{1,3},{2,0},{3,1},{4,6},{5,7},{6,4},{7,5},{8,10},{9,11},{10,... | collective-permute-start | bytes 152 | tf_op jit(solution)/shard_map/ppermute | solution.py:121
  8.8 6.9 %collective-permute-start.2 = (f32[3,4]{1,0:T(4,128)S(1)}, f32[3,4]{1,0:T(4,128)S(1)}, u32[]{:S(2)}, u32[]{:S(2)}) collective-permute-start(f32[3,4]{1,0:T(4,128)S(1)} %pad_maximum_fusion.1), channel_id=1, source_target_pairs={{0,3},{1,2},{2,1},{3,0},{4,7},{5,6},{6,5},{7,4},{8,11},{9,10},{10,... | collective-permute-start | bytes 152 | tf_op jit(solution)/shard_map/ppermute | solution.py:121
  10.9 12.1 %copy-start.14 = (f32[1,64,128]{2,1,0:T(8,128)S(1)}, f32[1,64,128]{2,1,0:T(8,128)}, u32[]{:S(2)}) copy-start(f32[1,64,128]{2,1,0:T(8,128)} %param.12) | copy-start | bytes 98308
  15.8 3.6 %collective-permute-start.3 = (f32[3,16]{1,0:T(4,128)S(1)}, f32[3,16]{1,0:T(4,128)S(1)}, u32[]{:S(2)}, u32[]{:S(2)}) collective-permute-start(f32[3,16]{1,0:T(4,128)S(1)} %pad_maximum_fusion.2), channel_id=1, source_target_pairs={{0,4},{1,5},{2,6},{3,7},{4,0},{5,1},{6,2},{7,3},{8,12},{9,13},{10,... | collective-permute-start | bytes 584 | tf_op jit(solution)/shard_map/ppermute | solution.py:121
  16.4 5.1 %collective-permute-start.4 = (f32[3,16]{1,0:T(4,128)S(1)}, f32[3,16]{1,0:T(4,128)S(1)}, u32[]{:S(2)}, u32[]{:S(2)}) collective-permute-start(f32[3,16]{1,0:T(4,128)S(1)} %pad_maximum_fusion.2), channel_id=1, source_target_pairs={{0,8},{1,9},{2,10},{3,11},{4,12},{5,13},{6,14},{7,15},{8,0},{9,1},... | collective-permute-start | bytes 584 | tf_op jit(solution)/shard_map/ppermute | solution.py:121
  18.8 3.6 %collective-permute-start.5 = (f32[3,16]{1,0:T(4,128)S(1)}, f32[3,16]{1,0:T(4,128)S(1)}, u32[]{:S(2)}, u32[]{:S(2)}) collective-permute-start(f32[3,16]{1,0:T(4,128)S(1)} %pad_maximum_fusion.2), channel_id=1, source_target_pairs={{0,12},{1,13},{2,14},{3,15},{4,8},{5,9},{6,10},{7,11},{8,4},{9,5},... | collective-permute-start | bytes 584 | tf_op jit(solution)/shard_map/ppermute | solution.py:121
  23.1 6.6 %copy-start.12 = (f32[128,8,8]{0,2,1:T(8,128)}, f32[128,8,8]{0,2,1:T(8,128)S(1)}, u32[]{:S(2)}) copy-start(f32[128,8,8]{0,2,1:T(8,128)S(1)} %fusion.90) | copy-start | bytes 98308
  29.8 6.2 %copy-start.17 = (f32[64]{0:T(128)S(1)}, f32[64]{0:T(128)}, u32[]{:S(2)}) copy-start(f32[64]{0:T(128)} %copy-done.16) | copy-start | bytes 772
  37.5 25.8 %copy-start.8 = (f32[128,64]{0,1:T(8,128)}, f32[128,64]{0,1:T(8,128)S(1)}, u32[]{:S(2)}) copy-start(f32[128,64]{0,1:T(8,128)S(1)} %get-tuple-element.92) | copy-start | bytes 98308
  49.9 49.7 %all-to-all-start = ((f32[16,264,128]{2,1,0:T(8,128)}), f32[16,264,128]{2,1,0:T(8,128)}, u32[]{:S(2)}, u32[]{:S(2)}) async-start(f32[16,264,128]{2,1,0:T(8,128)} %maximum_maximum_fusion), calls=%async_computation | async-start | bytes 4325376 | tf_op jit(solution)/shard_map/all_to_all | solution.py:93
  56.4 6.9 %copy-start.25 = (f32[64]{0:T(128)S(1)}, f32[64]{0:T(128)}, u32[]{:S(2)}) copy-start(f32[64]{0:T(128)} %get-tuple-element.105) | copy-start | bytes 772
  114.2 52.9 %all-to-all-start.1 = ((f32[16,256,128]{2,1,0:T(8,128)}), f32[16,256,128]{2,1,0:T(8,128)}, u32[]{:S(2)}, u32[]{:S(2)}) async-start(f32[16,256,128]{2,1,0:T(8,128)} %pad_maximum_fusion), calls=%async_computation.1 | async-start | bytes 4194304 | tf_op jit(solution)/shard_map/all_to_all | solution.py:112
  175.8 7.0 %copy-start.4 = (f32[128,8,64]{0,2,1:T(8,128)S(1)}, f32[128,8,64]{0,2,1:T(8,128)}, u32[]{:S(2)}) copy-start(f32[128,8,64]{0,2,1:T(8,128)} %convert_element_type.94) | copy-start | bytes 786436
  177.1 14.1 %copy-start.21 = (f32[64]{0:T(128)}, f32[64]{0:T(128)S(1)}, u32[]{:S(2)}) copy-start(f32[64]{0:T(128)S(1)} %get-tuple-element.88) | copy-start | bytes 772
  194.8 16.5 %copy-start.5 = (f32[128,8,64]{0,2,1:T(8,128)S(1)}, f32[128,8,64]{0,2,1:T(8,128)}, u32[]{:S(2)}) copy-start(f32[128,8,64]{0,2,1:T(8,128)} %convolution_bitcast_fusion) | copy-start | bytes 786436
  201.2 18.3 %all-to-all-start.2 = ((f32[16,3,4]{2,1,0:T(4,128)}), f32[16,3,4]{2,1,0:T(4,128)}, u32[]{:S(2)}, u32[]{:S(2)}) async-start(f32[16,3,4]{2,1,0:T(4,128)} %copy.156), calls=%async_computation.2 | async-start | bytes 65536 | tf_op jit(solution)/shard_map/all_to_all | solution.py:180
  220.3 5.2 %collective-permute-start.6 = (f32[3,4]{1,0:T(4,128)S(1)}, f32[3,4]{1,0:T(4,128)S(1)}, u32[]{:S(2)}, u32[]{:S(2)}) collective-permute-start(f32[3,4]{1,0:T(4,128)S(1)} %reduce_sum.197), channel_id=1, source_target_pairs={{0,16},{16,0},{32,48},{48,32},{64,80},{80,64},{96,112},{112,96},{1... | collective-permute-start | bytes 152 | tf_op jit(solution)/shard_map/ppermute | solution.py:121
  220.7 6.4 %collective-permute-start.7 = (f32[3,4]{1,0:T(4,128)S(1)}, f32[3,4]{1,0:T(4,128)S(1)}, u32[]{:S(2)}, u32[]{:S(2)}) collective-permute-start(f32[3,4]{1,0:T(4,128)S(1)} %reduce_sum.197), channel_id=1, source_target_pairs={{0,32},{16,48},{32,0},{48,16},{64,96},{80,112},{96,64},{112,80},{1... | collective-permute-start | bytes 152 | tf_op jit(solution)/shard_map/ppermute | solution.py:121
  225.5 4.8 %collective-permute-start.8 = (f32[3,4]{1,0:T(4,128)S(1)}, f32[3,4]{1,0:T(4,128)S(1)}, u32[]{:S(2)}, u32[]{:S(2)}) collective-permute-start(f32[3,4]{1,0:T(4,128)S(1)} %reduce_sum.197), channel_id=1, source_target_pairs={{0,48},{16,32},{32,16},{48,0},{64,112},{80,96},{96,80},{112,64},{1... | collective-permute-start | bytes 152 | tf_op jit(solution)/shard_map/ppermute | solution.py:121
  230.3 7.6 %collective-permute-start.10 = (f32[3,4]{1,0:T(4,128)S(1)}, f32[3,4]{1,0:T(4,128)S(1)}, u32[]{:S(2)}, u32[]{:S(2)}) collective-permute-start(f32[3,4]{1,0:T(4,128)S(1)} %add_add_fusion.1), channel_id=1, source_target_pairs={{0,128},{16,144},{32,160},{48,176},{64,192},{80,208},{96,224},{112... | collective-permute-start | bytes 152 | tf_op jit(solution)/shard_map/ppermute | solution.py:121
  234.9 5.4 %collective-permute-start.11 = (f32[3,4]{1,0:T(4,128)S(1)}, f32[3,4]{1,0:T(4,128)S(1)}, u32[]{:S(2)}, u32[]{:S(2)}) collective-permute-start(f32[3,4]{1,0:T(4,128)S(1)} %add_add_fusion.1), channel_id=1, source_target_pairs={{0,192},{16,208},{32,224},{48,240},{64,128},{80,144},{96,160},{112... | collective-permute-start | bytes 152 | tf_op jit(solution)/shard_map/ppermute | solution.py:121
  238.0 3.6 %collective-permute-start.9 = (f32[3,4]{1,0:T(4,128)S(1)}, f32[3,4]{1,0:T(4,128)S(1)}, u32[]{:S(2)}, u32[]{:S(2)}) collective-permute-start(f32[3,4]{1,0:T(4,128)S(1)} %add_add_fusion.1), channel_id=1, source_target_pairs={{0,64},{16,80},{32,96},{48,112},{64,0},{80,16},{96,32},{112,48},{1... | collective-permute-start | bytes 152 | tf_op jit(solution)/shard_map/ppermute | solution.py:121
  (20 other events, 71.4 us)
